TPU v7x, 256 devices: a whole 4x4x8 slice. The times are simulated.
256 devices in a mesh: blk: 16 (over z, x_lo), dp: 16 (over x_hi, y, core).
Axes of the slice: x: 4 (x_hi: 2, x_lo: 2; x = x_hi * 2 + x_lo), y: 4, z: 8, core: 2. Of those that a mesh axis runs over, the one named last changes fastest.
Arguments:
- audio_frames: bfloat16 [16, 1024, 16, 1024], P('dp', 'blk'), may hold values from -6 to 6
- conv_weight: bfloat16 [3072, 1024], replicated, may hold values from -0.109375 to 0.109375
- proj_weight: bfloat16 [1024, 512], replicated, may hold values from -0.1875 to 0.1875
- text_embed: bfloat16 [16, 1024, 512], P('dp', 'blk'), may hold values from -6 to 6
- pair_langs: int32 [16, 1024], P('dp', 'blk'), may hold values from 0 to 99, as said below
- log_scale: float32 [100], replicated, may hold values from 2 to 5
- lang_bias: float32 [100], replicated, may hold values from 95 to 105
- log_var: float32 [100], replicated, may hold values from -1 to 1
Outputs:
- loss: float32 [], replicated
- scale_grad: float32 [100], replicated
- var_grad: float32 [100], replicated
- conv_grad: float32 [3072, 1024], P('blk', 'dp')
- proj_grad: float32 [1024, 512], P('blk', 'dp')
- text_grad: float32 [16, 1024, 512], P('dp', 'blk')
Inputs may be any that keep to these rules, and one draw needn't show every extreme that they name: `pair_langs`: language ids of the pairs; in every draw some languages are named by no pair.
All inputs are finite; a program needn't handle non-finite values.
Results may differ from a plain program's by a relative error of at most 0.029.
Values may be sent and summed in bfloat16 or wider, within the bound.
No kernel may reach another device: no remote copies, remote signals or barrier semaphores. Data moves between devices by JAX's collectives and lax.ppermute only.
A program may use at most 128 MiB of HBM per device.

v0:
```python
import jax
import jax.numpy as jnp
from jax import lax
from jax.sharding import PartitionSpec as P

epsilon = 1e-06


def stack_taps(frames):
    clips, steps_count, channels = frames.shape
    blank = jnp.zeros_like(frames[:, :1])
    before = jnp.concatenate([blank, frames[:, :-1]], axis=1)
    after = jnp.concatenate([frames[:, 1:], blank], axis=1)
    return jnp.concatenate([before, frames, after], axis=2).reshape(
        clips * steps_count, 3 * channels
    )


def encode(frames, conv_weight, proj_weight):
    clips, steps_count, channels = frames.shape
    stacked = stack_taps(frames)
    preact = jnp.dot(stacked, conv_weight, preferred_element_type=jnp.float32)
    pooled = jnp.mean(jax.nn.gelu(preact).reshape(clips, steps_count, -1), axis=1).astype(
        jnp.bfloat16
    )
    embedding = jnp.dot(pooled, proj_weight, preferred_element_type=jnp.float32)
    audio_len = jnp.sqrt(jnp.sum(embedding * embedding, axis=-1, keepdims=True) + epsilon)
    return (stacked, preact, pooled, embedding / audio_len, audio_len)


def normalize_text(text_rows):
    text_float = text_rows.astype(jnp.float32)
    text_len = jnp.sqrt(jnp.sum(text_float * text_float, axis=-1, keepdims=True) + epsilon)
    return (text_float / text_len, text_len)


def encode_back(stacked, preact, pooled, audio_unit, audio_len, grad_audio, proj_weight):
    clips = pooled.shape[0]
    steps_count = preact.shape[0] // clips
    radial = jnp.sum(audio_unit * grad_audio, axis=-1, keepdims=True)
    grad_embed = ((grad_audio - audio_unit * radial) / audio_len).astype(jnp.bfloat16)
    proj_term = lax.dot_general(
        pooled, grad_embed, (((0,), (0,)), ((), ())), preferred_element_type=jnp.float32
    )
    grad_pooled = (
        lax.dot_general(
            grad_embed, proj_weight, (((1,), (1,)), ((), ())), preferred_element_type=jnp.float32
        )
        / steps_count
    )
    grad_act = jnp.broadcast_to(
        grad_pooled[:, None, :], (clips, steps_count, grad_pooled.shape[1])
    ).reshape(clips * steps_count, -1)
    grad_pre = jax.vjp(jax.nn.gelu, preact)[1](grad_act)[0].astype(jnp.bfloat16)
    conv_term = lax.dot_general(
        stacked, grad_pre, (((0,), (0,)), ((), ())), preferred_element_type=jnp.float32
    )
    return (conv_term, proj_term)


def local(
    audio_frames, conv_weight, proj_weight, text_embed, pair_langs, log_scale, lang_bias, log_var
):
    frames = audio_frames[0]
    text_rows = text_embed[0]
    pair_ids = pair_langs[0]
    local_pairs = frames.shape[0]
    classes = jnp.arange(log_scale.shape[0], dtype=jnp.int32)
    onehot = (pair_ids[:, None] == classes[None, :]).astype(jnp.float32)
    counts = lax.psum(jnp.sum(onehot, axis=0), ("blk", "dp"))
    weight_table = jnp.exp(-log_var) / jnp.maximum(counts, 1.0)
    scale_table = jnp.exp(log_scale)
    stacked, preact, pooled, audio_unit, audio_len = encode(frames, conv_weight, proj_weight)
    audio_bf = audio_unit.astype(jnp.bfloat16)
    text_unit, text_len = normalize_text(text_rows)
    text_bf = text_unit.astype(jnp.bfloat16)
    all_text = lax.all_gather(text_bf, "blk", axis=0, tiled=True)
    all_ids = lax.all_gather(pair_ids, "blk", axis=0, tiled=True)
    pair_scale = jnp.sum(onehot * scale_table[None, :], axis=1)
    pair_bias = jnp.sum(onehot * lang_bias[None, :], axis=1)
    own_weight = jnp.sum(onehot * weight_table[None, :], axis=1)
    all_onehot = (all_ids[:, None] == classes[None, :]).astype(jnp.float32)
    col_weight = jnp.sum(all_onehot * weight_table[None, :], axis=1)
    logits = (
        pair_scale[:, None]
        * lax.dot_general(
            audio_bf, all_text, (((1,), (1,)), ((), ())), preferred_element_type=jnp.float32
        )
        + pair_bias[:, None]
    )
    row_max = jnp.max(logits, axis=1)
    row_lse = row_max + jnp.log(jnp.sum(jnp.exp(logits - row_max[:, None]), axis=1))
    local_max = jnp.max(logits, axis=0)
    joint_max = lax.pmax(local_max, "blk")
    joint_sum = lax.psum(jnp.sum(jnp.exp(logits - joint_max[None, :]), axis=0), "blk")
    col_lse = joint_max + jnp.log(joint_sum)
    offset = lax.axis_index("blk") * local_pairs
    own_cols = lax.dynamic_slice_in_dim(logits, offset, local_pairs, 1)
    positive = jnp.diagonal(own_cols)
    own_col_lse = lax.dynamic_slice_in_dim(col_lse, offset, local_pairs, 0)
    pair_loss = 0.5 * (row_lse + own_col_lse) - positive
    local_index = jnp.arange(local_pairs, dtype=jnp.int32)
    all_index = jnp.arange(logits.shape[1], dtype=jnp.int32)
    on_diagonal = all_index[None, :] == (offset + local_index)[:, None]
    score_grad = 0.5 * (
        own_weight[:, None] * jnp.exp(logits - row_lse[:, None])
        + col_weight[None, :] * jnp.exp(logits - col_lse[None, :])
    )
    score_grad = score_grad - jnp.where(on_diagonal, own_weight[:, None], 0.0)
    scale_terms = jnp.sum(score_grad * (logits - pair_bias[:, None]), axis=1)
    weighted = (score_grad * pair_scale[:, None]).astype(jnp.bfloat16)
    grad_audio = jnp.dot(weighted, all_text, preferred_element_type=jnp.float32)
    grad_text = lax.psum_scatter(
        lax.dot_general(
            weighted, audio_bf, (((0,), (0,)), ((), ())), preferred_element_type=jnp.float32
        ).astype(jnp.bfloat16),
        "blk",
        scatter_dimension=0,
        tiled=True,
    ).astype(jnp.float32)
    text_grad = (
        grad_text - text_unit * jnp.sum(text_unit * grad_text, axis=1, keepdims=True)
    ) / text_len
    conv_term, proj_term = encode_back(
        stacked, preact, pooled, audio_unit, audio_len, grad_audio, proj_weight
    )
    loss_sum, scale_grad = lax.psum(
        (
            jnp.sum(onehot * pair_loss[:, None], axis=0),
            jnp.sum(onehot * scale_terms[:, None], axis=0),
        ),
        ("blk", "dp"),
    )
    conv_half, proj_half = (
        lax.psum_scatter(
            conv_term.astype(jnp.bfloat16), "dp", scatter_dimension=1, tiled=True
        ).astype(jnp.float32),
        lax.psum_scatter(
            proj_term.astype(jnp.bfloat16), "dp", scatter_dimension=1, tiled=True
        ).astype(jnp.float32),
    )
    conv_grad, proj_grad = (
        lax.psum_scatter(
            conv_half.astype(jnp.bfloat16), "blk", scatter_dimension=0, tiled=True
        ).astype(jnp.float32),
        lax.psum_scatter(
            proj_half.astype(jnp.bfloat16), "blk", scatter_dimension=0, tiled=True
        ).astype(jnp.float32),
    )
    var_weight = jnp.exp(-log_var)
    lang_mean = loss_sum / jnp.maximum(counts, 1.0)
    loss = jnp.sum(var_weight * lang_mean + log_var)
    var_grad = 1.0 - var_weight * lang_mean
    return (loss, scale_grad, var_grad, conv_grad, proj_grad, text_grad[None])


def solution(mesh):
    return jax.shard_map(
        local,
        mesh=mesh,
        in_specs=(
            P("dp", "blk", None, None),
            P(),
            P(),
            P("dp", "blk", None),
            P("dp", "blk"),
            P(),
            P(),
            P(),
        ),
        out_specs=(P(), P(), P(), P("blk", "dp"), P("blk", "dp"), P("dp", "blk", None)),
        check_vma=False,
    )
```

profile of v0, /device:TPU:8, one launch (start us, length us, event | category | flops | bytes accessed | tf_op | source)
XLA Modules:
  0.0 605.4 jit_solution(14291280463553206646)
XLA Ops:
  7.2 1.0 fusion.15
  8.3 0.6 copy-done.8
  8.9 1.6 fusion.23
  10.5 3.3 fusion.26
  13.9 2.3 concatenate.20
  16.1 1.7 concatenate.23
  17.9 78.8 %psum.30 = f32[100]{0:T(128)S(1)} all-reduce(f32[100]{0:T(128)S(1)} %convert_reduce_fusion), channel_id=1, replica_groups=mesh['blk'=16,'dp'=16] {'blk','dp'}, use_global_device_ids=true, to_apply=%region_14.0 | all-reduce | flops 100 | bytes 800 | tf_op jit(solution)/shard_map/psum | solution.py:70
  96.8 0.5 iota_add_fusion
  97.3 0.6 dynamic-slice
  98.6 0.1 bitcast_dynamic-update-slice_fusion
  98.7 14.4 %all-reduce.2 = s32[1024]{0:T(1024)S(1)} all-reduce(s32[1024]{0:T(1024)S(1)} %bitcast_dynamic-update-slice_fusion), channel_id=2, replica_groups=mesh['blk'=16,'dp'=16] {'blk'}, use_global_device_ids=true, to_apply=%add.2 | all-reduce | flops 1024 | bytes 8192
  113.1 0.1 select_reduce_fusion
  113.3 0.7 select_reduce_fusion.2
  114.0 12.8 %bitcast_reduce_fusion = (f32[64,1024]{1,0:T(8,128)S(1)}, f32[1024,1024]{1,0:T(8,128)}) fusion(bf16[3072,1024]{1,0:T(8,128)(2,1)} %param.9, bf16[1024,1024]{1,0:T(8,128)(2,1)} %bitcast.49, bf16[1024,1024]{1,0:T(8,128)(2,1)S(1)} %bitcast.45, bf16[1024,1024]{1,0:T(8,128)(2,1)} %bitcast.47), kind=kOutput, calls=%fused_computation.17 | convolution fusion | flops 6470696960 | bytes 17039360 | tf_op jit(solution)/shard_map/dot_general | solution.py:22
  126.8 0.4 multiply_reduce_fusion.2
  127.2 0.6 add_sqrt_fusion.1
  127.7 2.3 fusion.25
  130.1 33.1 %pmax.7 = f32[1024]{0:T(1024)S(1)} all-reduce(f32[1024]{0:T(1024)S(1)} %get-tuple-element.8), channel_id=1, replica_groups=mesh['blk'=16,'dp'=16] {'blk'}, use_global_device_ids=true, to_apply=%region_8.0 | all-reduce | flops 1024 | bytes 8192 | tf_op jit(solution)/shard_map/pmax | solution.py:94
  163.1 1.5 exponential_reduce_fusion
  164.6 31.2 %psum.28 = f32[1024]{0:T(1024)} all-reduce(f32[1024]{0:T(1024)S(1)} %get-tuple-element.6), channel_id=1, replica_groups=mesh['blk'=16,'dp'=16] {'blk'}, use_global_device_ids=true, to_apply=%region_10.0 | all-reduce | flops 1024 | bytes 8192 | tf_op jit(solution)/shard_map/psum | solution.py:95
  195.8 0.7 log_add_fusion
  196.5 0.8 gather_fusion
  197.4 1.3 multiply_subtract_fusion
  198.6 1.7 multiply_reduce_fusion.1
  200.4 0.6 copy-done.21
  201.0 2.6 convolution_convert_fusion.2
  203.6 2.1 convolution_multiply_fusion
  205.7 0.2 reduce-scatter.10.cloned.1.call-start
  205.9 4.6 fusion.6
  210.6 9.3 %convolution_convert_fusion = bf16[3072,1024]{0,1:T(8,128)(2,1)} fusion(bf16[1024,1024]{1,0:T(8,128)(2,1)S(1)} %fusion.6, bf16[1024,1024]{1,0:T(8,128)(2,1)S(1)} %bitcast.50, bf16[1024,1024]{1,0:T(8,128)(2,1)S(1)} %bitcast.46, bf16[1024,1024]{1,0:T(8,128)(2,1)S(1)} %bitcast.48), kind=kOutput, calls=%fused_computation.6 | convolution fusion | flops 6464471040 | bytes 14680064 | tf_op jit(solution)/shard_map/dot_general | solution.py:55
  220.0 57.6 %reduce-scatter.12.cloned.1.call-done = bf16[1024,32]{0,1:T(8,128)(2,1)} async-done(((bf16[1024,512]{0,1:T(8,128)(2,1)}), bf16[1024,32]{0,1:T(8,128)(2,1)}) %reduce-scatter.12.cloned.1.call-update) | async-done | bytes 65552 | tf_op jit(solution)/shard_map/reduce_scatter | solution.py:138
  277.6 1.7 copy.16
  279.4 1.6 convolution_convert_fusion.1
  281.1 0.3 multiply_reduce_fusion
  281.4 97.4 %reduce-scatter.10.cloned.1.call-done = bf16[3072,64]{0,1:T(8,128)(2,1)} async-done(((bf16[3072,1024]{0,1:T(8,128)(2,1)}), bf16[3072,64]{0,1:T(8,128)(2,1)}) %reduce-scatter.10.cloned.1.call-update) | async-done | bytes 393232 | tf_op jit(solution)/shard_map/reduce_scatter | solution.py:135
  378.7 2.1 copy.14
  380.9 0.1 select_reduce_fusion.1
  381.0 74.3 %all-reduce.3 = (f32[100]{0:T(128)S(1)}, f32[100]{0:T(128)}) all-reduce(f32[100]{0:T(128)S(1)} %get-tuple-element.11, f32[100]{0:T(128)S(1)} %get-tuple-element.10), channel_id=1, replica_groups=mesh['blk'=16,'dp'=16] {'blk','dp'}, use_global_device_ids=true, to_apply=%region_12.0 | all-reduce | flops 200 | bytes 1600 | tf_op jit(solution)/shard_map/psum | solution.py:127
  455.3 0.5 broadcast_subtract_fusion
  455.8 0.6 add_reduce_fusion
  456.4 0.8 copy.17
  457.2 0.6 convert_element_type.62
  457.9 66.6 %reduce-scatter.14.cloned.1.call-done = bf16[64,512]{1,0:T(8,128)(2,1)} async-done(((bf16[1024,512]{1,0:T(8,128)(2,1)}), bf16[64,512]{1,0:T(8,128)(2,1)}) %reduce-scatter.14.cloned.1.call-update) | async-done | bytes 65552 | tf_op jit(solution)/shard_map/reduce_scatter | solution.py:113
  524.5 1.0 fusion.12
  525.5 1.6 fusion.14
  527.1 69.9 %reduce-scatter.16.cloned.1.call-done = bf16[192,64]{1,0:T(8,128)(2,1)} async-done(((bf16[3072,64]{1,0:T(8,128)(2,1)}), bf16[192,64]{1,0:T(8,128)(2,1)}) %reduce-scatter.16.cloned.1.call-update) | async-done | bytes 24592
  597.0 0.9 copy.15
  597.9 0.6 convert_element_type.60
  (76 shorter events, 0.6 us)
Async XLA Ops:
  7.2 119.6 %copy-start = (bf16[1024,512]{1,0:T(8,128)(2,1)S(1)}, bf16[1024,512]{1,0:T(8,128)(2,1)}, u32[]{:S(2)}) copy-start(bf16[1024,512]{1,0:T(8,128)(2,1)} %param.10) | copy-start | bytes 3145732
  7.2 120.5 %all-gather.3.cloned.1.call-start = ((), (), s32[]{:S(2)}) async-start(), calls=%async_computation.5 | async-start | bytes 1114112 | tf_op jit(solution)/shard_map/all_gather | solution.py:77
  8.3 0.6 copy-start.8
  10.5 267.1 %reduce-scatter.12.cloned.1.call-start = ((), (), s32[]{:S(2)}) async-start(), calls=%async_computation.7 | async-start | bytes 1114112 | tf_op jit(solution)/shard_map/reduce_scatter | solution.py:138
  13.8 4.1 copy-start.17
  13.8 83.0 %copy-start.27 = (f32[100]{0:T(128)S(1)}, f32[100]{0:T(128)}, u32[]{:S(2)}) copy-start(f32[100]{0:T(128)} %param.13) | copy-start | bytes 1204
  13.8 83.5 %copy-start.28 = (u32[256]{0:T(256)S(1)}, u32[256]{0:T(256)}, u32[]{:S(2)}) copy-start(u32[256]{0:T(256)} %constant.71) | copy-start | bytes 3076
  13.8 99.3 %copy-start.23 = (f32[100]{0:T(128)S(1)}, f32[100]{0:T(128)}, u32[]{:S(2)}) copy-start(f32[100]{0:T(128)} %param.15) | copy-start | bytes 1204
  13.8 99.4 %copy-start.22 = (f32[100]{0:T(128)S(1)}, f32[100]{0:T(128)}, u32[]{:S(2)}) copy-start(f32[100]{0:T(128)} %param.14) | copy-start | bytes 1204
  13.9 100.1 %copy-start.1 = (bf16[1,64,16,1024]{3,2,1,0:T(8,128)(2,1)S(1)}, bf16[1,64,16,1024]{3,2,1,0:T(8,128)(2,1)}, u32[]{:S(2)}) copy-start(bf16[1,64,16,1024]{3,2,1,0:T(8,128)(2,1)} %param.8) | copy-start | bytes 6291460
  96.8 30.0 %copy-start.25 = (f32[100]{0:T(128)}, f32[100]{0:T(128)S(1)}, u32[]{:S(2)}) copy-start(f32[100]{0:T(128)S(1)} %psum.30) | copy-start | bytes 1204
  114.0 13.8 %copy-start.10 = (f32[64]{0:T(128)}, f32[64]{0:T(128)S(1)}, u32[]{:S(2)}) copy-start(f32[64]{0:T(128)S(1)} %get-tuple-element.13) | copy-start | bytes 772
  126.8 1.0 copy-start.7
  127.2 68.6 %copy-start.4 = (f32[64,512]{1,0:T(8,128)}, f32[64,512]{1,0:T(8,128)S(1)}, u32[]{:S(2)}) copy-start(f32[64,512]{1,0:T(8,128)S(1)} %get-tuple-element.26) | copy-start | bytes 393220
  196.5 7.1 %copy-start.12 = (f32[64]{0:T(128)S(1)}, f32[64]{0:T(128)}, u32[]{:S(2)}) copy-start(f32[64]{0:T(128)} %add_sqrt_fusion.1) | copy-start | bytes 772
  198.6 11.9 %copy-start.15 = (f32[64]{0:T(128)}, f32[64]{0:T(128)S(1)}, u32[]{:S(2)}) copy-start(f32[64]{0:T(128)S(1)} %get-tuple-element.20) | copy-start | bytes 772
  200.4 0.6 copy-start.21
  205.7 173.0 %reduce-scatter.10.cloned.1.call-start = ((), (), s32[]{:S(2)}) async-start(), calls=%async_computation.6 | async-start | bytes 6684672 | tf_op jit(solution)/shard_map/reduce_scatter | solution.py:135
  205.9 4.6 copy-start.2
  205.9 4.6 copy-start.3
  219.8 59.5 %copy-start.5 = (f32[64,512]{1,0:T(8,128)S(1)}, f32[64,512]{1,0:T(8,128)}, u32[]{:S(2)}) copy-start(f32[64,512]{1,0:T(8,128)} %copy-done.4) | copy-start | bytes 393220
  219.8 59.5 %copy-start.13 = (f32[64]{0:T(128)S(1)}, f32[64]{0:T(128)}, u32[]{:S(2)}) copy-start(f32[64]{0:T(128)} %get-tuple-element.12) | copy-start | bytes 772
  219.8 59.5 %copy-start.14 = (f32[64]{0:T(128)S(1)}, f32[64]{0:T(128)}, u32[]{:S(2)}) copy-start(f32[64]{0:T(128)} %get-tuple-element.14) | copy-start | bytes 772
  219.8 59.5 %copy-start.16 = (f32[64]{0:T(128)S(1)}, f32[64]{0:T(128)}, u32[]{:S(2)}) copy-start(f32[64]{0:T(128)} %copy-done.15) | copy-start | bytes 772
  219.8 59.5 %copy-start.20 = (s32[64]{0:T(128)S(1)}, s32[64]{0:T(128)}, u32[]{:S(2)}) copy-start(s32[64]{0:T(128)} %iota_add_fusion) | copy-start | bytes 772
  219.9 61.2 %copy-start.11 = (f32[64]{0:T(128)S(1)}, f32[64]{0:T(128)}, u32[]{:S(2)}) copy-start(f32[64]{0:T(128)} %copy-done.10) | copy-start | bytes 772
  219.9 161.0 %copy-start.18 = (s32[1,64]{1,0:T(1,128)S(1)}, s32[1,64]{1,0:T(1,128)}, u32[]{:S(2)}) copy-start(s32[1,64]{1,0:T(1,128)} %param.12) | copy-start | bytes 772
  219.9 161.0 %copy-start.19 = (f32[64]{0:T(128)S(1)}, f32[64]{0:T(128)}, u32[]{:S(2)}) copy-start(f32[64]{0:T(128)} %get-tuple-element.19) | copy-start | bytes 772
  219.9 235.4 %copy-start.24 = (f32[100]{0:T(128)S(1)}, f32[100]{0:T(128)}, u32[]{:S(2)}) copy-start(f32[100]{0:T(128)} %param.15) | copy-start | bytes 1204
  219.9 235.4 %copy-start.26 = (f32[100]{0:T(128)S(1)}, f32[100]{0:T(128)}, u32[]{:S(2)}) copy-start(f32[100]{0:T(128)} %copy-done.25) | copy-start | bytes 1204
  219.9 304.5 %copy-start.6 = (bf16[1,64,512]{2,1,0:T(8,128)(2,1)S(1)}, bf16[1,64,512]{2,1,0:T(8,128)(2,1)}, u32[]{:S(2)}) copy-start(bf16[1,64,512]{2,1,0:T(8,128)(2,1)} %param.11) | copy-start | bytes 196612
  219.9 304.5 %copy-start.9 = (f32[64]{0:T(128)S(1)}, f32[64]{0:T(128)}, u32[]{:S(2)}) copy-start(f32[64]{0:T(128)} %copy-done.8) | copy-start | bytes 772
  220.0 236.5 %reduce-scatter.18.cloned.1.call-start = ((), (), s32[]{:S(2)}) async-start(), calls=%async_computation.10 | async-start | bytes 278528
  279.3 245.2 %reduce-scatter.14.cloned.1.call-start = ((), (), s32[]{:S(2)}) async-start(), calls=%async_computation.8 | async-start | bytes 1114112 | tf_op jit(solution)/shard_map/reduce_scatter | solution.py:113
  281.0 316.0 %reduce-scatter.16.cloned.1.call-start = ((), (), s32[]{:S(2)}) async-start(), calls=%async_computation.9 | async-start | bytes 835584
Sparse Core Ops, SparseCore 0:
  10.6 71.0 all-gather.2
  205.8 71.7 reduce-scatter.11
  282.1 96.6 reduce-scatter.9
  381.1 70.0 reduce-scatter.17
  453.5 70.8 reduce-scatter.13
  526.8 70.1 reduce-scatter.15
where the time goes:
time: 606 us; the launch traced here: 605 us
  waiting for transfers between devices  292 us (48%)
  blocking collectives  232 us (38%)
  matrix products  32.8 us (5%)
  other arithmetic  18 us (3%)
  local copies, waits for them, and re-layouts  15.6 us (3%)
  between operations  15.1 us (2%)
    reduce_scatter x1, waiting for transfers between devices, local(): lax.psum_scatter(conv_term.astype(jnp.bfloat16), 'dp', scatter_dimension=...  97.4 us
    psum x1, blocking collectives, local(): counts = lax.psum(jnp.sum(onehot, axis=0), ('blk', 'dp'))  78.8 us
    psum x1, blocking collectives, local(): lax.psum((jnp.sum(onehot * pair_loss[:, None], axis=0), jnp.sum(onehot *...  74.3 us
    unnamed x8, waiting for transfers between devices  70 us
    reduce_scatter x1, waiting for transfers between devices, local(): lax.psum_scatter(lax.dot_general(weighted, audio_bf, (((0,), (0,)), ((),...  66.6 us
    reduce_scatter x1, waiting for transfers between devices, local(): lax.psum_scatter(proj_term.astype(jnp.bfloat16), 'dp', scatter_dimension=...  57.6 us
    pmax x1, blocking collectives, local(): joint_max = lax.pmax(local_max, 'blk')  33.1 us
    psum x1, blocking collectives, local(): lax.psum(jnp.sum(jnp.exp(logits - joint_max[None, :]), axis=0), 'blk')  31.2 us
  transfers between devices with their start and end apart: 6, of which 4 were waited for; matrix products, arithmetic and copies ran while one was open for 8% of the time, Pallas kernels for 0%

commit v1 on v0

v1 whole, which is shorter than its diff:
```python
import jax
import jax.numpy as jnp
from jax import lax
from jax.sharding import PartitionSpec as P

epsilon = 1e-06


def stack_taps(frames):
    clips, steps_count, channels = frames.shape
    blank = jnp.zeros_like(frames[:, :1])
    before = jnp.concatenate([blank, frames[:, :-1]], axis=1)
    after = jnp.concatenate([frames[:, 1:], blank], axis=1)
    return jnp.concatenate([before, frames, after], axis=2).reshape(
        clips * steps_count, 3 * channels
    )


def encode(frames, conv_weight, proj_weight):
    clips, steps_count, channels = frames.shape
    stacked = stack_taps(frames)
    preact = jnp.dot(stacked, conv_weight, preferred_element_type=jnp.float32)
    pooled = jnp.mean(jax.nn.gelu(preact).reshape(clips, steps_count, -1), axis=1).astype(
        jnp.bfloat16
    )
    embedding = jnp.dot(pooled, proj_weight, preferred_element_type=jnp.float32)
    audio_len = jnp.sqrt(jnp.sum(embedding * embedding, axis=-1, keepdims=True) + epsilon)
    return (stacked, preact, pooled, embedding / audio_len, audio_len)


def normalize_text(text_rows):
    text_float = text_rows.astype(jnp.float32)
    text_len = jnp.sqrt(jnp.sum(text_float * text_float, axis=-1, keepdims=True) + epsilon)
    return (text_float / text_len, text_len)


def encode_back(stacked, preact, pooled, audio_unit, audio_len, grad_audio, proj_weight):
    clips = pooled.shape[0]
    steps_count = preact.shape[0] // clips
    radial = jnp.sum(audio_unit * grad_audio, axis=-1, keepdims=True)
    grad_embed = ((grad_audio - audio_unit * radial) / audio_len).astype(jnp.bfloat16)
    proj_term = lax.dot_general(
        pooled, grad_embed, (((0,), (0,)), ((), ())), preferred_element_type=jnp.float32
    )
    grad_pooled = (
        lax.dot_general(
            grad_embed, proj_weight, (((1,), (1,)), ((), ())), preferred_element_type=jnp.float32
        )
        / steps_count
    )
    grad_act = jnp.broadcast_to(
        grad_pooled[:, None, :], (clips, steps_count, grad_pooled.shape[1])
    ).reshape(clips * steps_count, -1)
    grad_pre = jax.vjp(jax.nn.gelu, preact)[1](grad_act)[0].astype(jnp.bfloat16)
    conv_term = lax.dot_general(
        stacked, grad_pre, (((0,), (0,)), ((), ())), preferred_element_type=jnp.float32
    )
    return (conv_term, proj_term)


def blocks_for_scatter(term, n_blk, n_dp):
    rows, cols = term.shape
    return (
        term.astype(jnp.bfloat16)
        .reshape(n_blk, rows // n_blk, n_dp, cols // n_dp)
        .transpose(2, 0, 1, 3)
        .reshape(n_dp, n_blk, (rows // n_blk) * (cols // n_dp))
    )


def local(
    audio_frames, conv_weight, proj_weight, text_embed, pair_langs, log_scale, lang_bias, log_var
):
    frames = audio_frames[0]
    text_rows = text_embed[0]
    pair_ids = pair_langs[0]
    local_pairs = frames.shape[0]
    n_blk = lax.axis_size("blk")
    n_dp = lax.axis_size("dp")
    emb = proj_weight.shape[1]
    classes = jnp.arange(log_scale.shape[0], dtype=jnp.int32)
    onehot = (pair_ids[:, None] == classes[None, :]).astype(jnp.float32)
    local_counts = jnp.sum(onehot, axis=0)
    stacked, preact, pooled, audio_unit, audio_len = encode(frames, conv_weight, proj_weight)
    audio_bf = audio_unit.astype(jnp.bfloat16)
    text_unit, text_len = normalize_text(text_rows)
    text_bf = text_unit.astype(jnp.bfloat16)
    id_cols = jnp.broadcast_to(pair_ids.astype(jnp.bfloat16)[:, None], (local_pairs, 128))
    packet = jnp.concatenate([audio_bf, text_bf, id_cols], axis=1)
    packet, local_counts = lax.optimization_barrier((packet, local_counts))
    gathered = lax.all_gather(packet, "blk", axis=0, tiled=True)
    counts = lax.psum(local_counts, ("blk", "dp"))
    all_audio = gathered[:, :emb]
    all_text = gathered[:, emb : 2 * emb]
    all_ids = gathered[:, 2 * emb].astype(jnp.int32)
    weight_table = jnp.exp(-log_var) / jnp.maximum(counts, 1.0)
    scale_table = jnp.exp(log_scale)
    all_onehot = (all_ids[:, None] == classes[None, :]).astype(jnp.float32)
    pair_scale = jnp.sum(all_onehot * scale_table[None, :], axis=1)
    pair_bias = jnp.sum(all_onehot * lang_bias[None, :], axis=1)
    pair_weight = jnp.sum(all_onehot * weight_table[None, :], axis=1)
    logits = (
        pair_scale[:, None]
        * lax.dot_general(
            all_audio, all_text, (((1,), (1,)), ((), ())), preferred_element_type=jnp.float32
        )
        + pair_bias[:, None]
    )
    row_max = jnp.max(logits, axis=1)
    row_lse = row_max + jnp.log(jnp.sum(jnp.exp(logits - row_max[:, None]), axis=1))
    col_max = jnp.max(logits, axis=0)
    col_lse = col_max + jnp.log(jnp.sum(jnp.exp(logits - col_max[None, :]), axis=0))
    positive = jnp.diagonal(logits)
    pair_loss = 0.5 * (row_lse + col_lse) - positive
    index = jnp.arange(logits.shape[0], dtype=jnp.int32)
    on_diagonal = index[:, None] == index[None, :]
    score_grad = 0.5 * (
        pair_weight[:, None] * jnp.exp(logits - row_lse[:, None])
        + pair_weight[None, :] * jnp.exp(logits - col_lse[None, :])
    )
    score_grad = score_grad - jnp.where(on_diagonal, pair_weight[:, None], 0.0)
    scale_terms = jnp.sum(score_grad * (logits - pair_bias[:, None]), axis=1)
    weighted = (score_grad * pair_scale[:, None]).astype(jnp.bfloat16)
    offset = lax.axis_index("blk") * local_pairs
    own_rows = lax.dynamic_slice_in_dim(weighted, offset, local_pairs, 0)
    own_cols = lax.dynamic_slice_in_dim(weighted, offset, local_pairs, 1)
    grad_audio = jnp.dot(own_rows, all_text, preferred_element_type=jnp.float32)
    grad_text = lax.dot_general(
        own_cols, all_audio, (((0,), (0,)), ((), ())), preferred_element_type=jnp.float32
    )
    text_grad = (
        grad_text - text_unit * jnp.sum(text_unit * grad_text, axis=1, keepdims=True)
    ) / text_len
    batch_sums = jnp.stack(
        [
            jnp.sum(all_onehot * pair_loss[:, None], axis=0),
            jnp.sum(all_onehot * scale_terms[:, None], axis=0),
        ]
    )
    conv_term, proj_term = encode_back(
        stacked, preact, pooled, audio_unit, audio_len, grad_audio, proj_weight
    )
    buf = jnp.concatenate(
        [blocks_for_scatter(conv_term, n_blk, n_dp), blocks_for_scatter(proj_term, n_blk, n_dp)],
        axis=2,
    )
    buf, batch_sums = lax.optimization_barrier((buf, batch_sums))
    stage = lax.psum_scatter(buf, "dp", scatter_dimension=0, tiled=True)
    stage = lax.psum_scatter(stage.reshape(n_blk, -1), "blk", scatter_dimension=0, tiled=True)
    loss_sum, scale_grad = lax.psum(batch_sums, "dp")
    conv_rows = conv_term.shape[0] // n_blk
    conv_cols = conv_term.shape[1] // n_dp
    conv_size = conv_rows * conv_cols
    conv_grad = stage[0, :conv_size].reshape(conv_rows, conv_cols).astype(jnp.float32)
    proj_grad = (
        stage[0, conv_size:]
        .reshape(proj_term.shape[0] // n_blk, proj_term.shape[1] // n_dp)
        .astype(jnp.float32)
    )
    var_weight = jnp.exp(-log_var)
    lang_mean = loss_sum / jnp.maximum(counts, 1.0)
    loss = jnp.sum(var_weight * lang_mean + log_var)
    var_grad = 1.0 - var_weight * lang_mean
    return (loss, scale_grad, var_grad, conv_grad, proj_grad, text_grad[None])


def solution(mesh):
    return jax.shard_map(
        local,
        mesh=mesh,
        in_specs=(
            P("dp", "blk", None, None),
            P(),
            P(),
            P("dp", "blk", None),
            P("dp", "blk"),
            P(),
            P(),
            P(),
        ),
        out_specs=(P(), P(), P(), P("blk", "dp"), P("blk", "dp"), P("dp", "blk", None)),
        check_vma=False,
    )
```

time: 606 us -> 493 us (0.81)
  blocking collectives: 232 us -> 111 us
  waiting for transfers between devices: 292 us -> 202 us
  local copies, waits for them, and re-layouts: 15.6 us -> 102 us
  other arithmetic: 18 us -> 29.3 us
    reduce_scatter x3 -> x1, waiting for transfers between devices: 222 us -> 64.4 us  [local(): stage = lax.psum_scatter(buf, 'dp', scatter_dimension=0, tiled=True)]
    psum x3 -> x2, blocking collectives: 184 us -> 111 us  [the longest x1 80.4 us: local(): counts = lax.psum(local_counts, ('blk', 'dp'))]
    unnamed x8 -> x4, waiting for transfers between devices: 70 us -> 137 us
    reshape x0 -> x4, local copies, waits for them, and re-layouts: none -> 39 us  [blocks_for_scatter(): return term.astype(jnp.bfloat16).reshape(n_blk, rows // n_blk, n_dp, cols...]
    pmax x1 -> x0, blocking collectives: 33.1 us -> none  [local(): joint_max = lax.pmax(local_max, 'blk')]
    gather x1, local copies, waits for them, and re-layouts: 0.81 us -> 21.2 us  [local(): positive = jnp.diagonal(logits)]
    transpose x0 -> x2, local copies, waits for them, and re-layouts: none -> 20.1 us  [blocks_for_scatter(): return term.astype(jnp.bfloat16).reshape(n_blk, rows // n_blk, n_dp, cols...]
    unnamed x1 -> x0, blocking collectives: 14.4 us -> none
  transfers between devices with their start and end apart: 6 -> 3, of which waited for: 4 -> 2; matrix products, arithmetic and copies ran while one was open for 8% -> 1% of each run, Pallas kernels for 0% -> 0%
where the time goes in v1:
time: 493 us; the launch traced here: 490 us
  waiting for transfers between devices  202 us (41%)
  blocking collectives  111 us (23%)
  local copies, waits for them, and re-layouts  102 us (21%)
  matrix products  32.3 us (7%)
  other arithmetic  29.3 us (6%)
  between operations  14.1 us (3%)
    unnamed x4, waiting for transfers between devices  137 us
    psum x1, blocking collectives, local(): counts = lax.psum(local_counts, ('blk', 'dp'))  80.4 us
    reduce_scatter x1, waiting for transfers between devices, local(): stage = lax.psum_scatter(buf, 'dp', scatter_dimension=0, tiled=True)  64.4 us
    reshape x4, local copies, waits for them, and re-layouts, blocks_for_scatter(): return term.astype(jnp.bfloat16).reshape(n_blk, rows // n_blk, n_dp, cols...  39 us
    psum x1, blocking collectives, local(): loss_sum, scale_grad = lax.psum(batch_sums, 'dp')  30.2 us
    gather x1, local copies, waits for them, and re-layouts, local(): positive = jnp.diagonal(logits)  21.2 us
    transpose x2, local copies, waits for them, and re-layouts, blocks_for_scatter(): return term.astype(jnp.bfloat16).reshape(n_blk, rows // n_blk, n_dp, cols...  20.1 us
    dot_general x1, matrix products, encode_back(): lax.dot_general(stacked, grad_pre, (((0,), (0,)), ((), ())), preferred_el...  10.7 us
  transfers between devices with their start and end apart: 3, of which 2 were waited for; matrix products, arithmetic and copies ran while one was open for 1% of the time, Pallas kernels for 0%

profile of v1, /device:TPU:8, one launch (start us, length us, event | category | flops | bytes accessed | tf_op | source)
XLA Modules:
  0.0 490.3 jit_solution(6311486120321933830)
XLA Ops:
  7.2 0.7 bitcast_convert_fusion
  8.0 1.3 convert_reduce_fusion.1
  9.2 1.0 fusion.18
  10.2 3.3 fusion.34
  13.5 0.9 concatenate.26
  15.1 3.3 copy-done.30
  18.4 9.5 %bitcast_reduce_fusion = (f32[64,1024]{1,0:T(8,128)S(1)}, f32[1024,1024]{1,0:T(8,128)}) fusion(bf16[3072,1024]{1,0:T(8,128)(2,1)S(1)} %copy-done.30, bf16[1024,1024]{1,0:T(8,128)(2,1)S(1)} %bitcast.67, bf16[1024,1024]{1,0:T(8,128)(2,1)S(1)} %bitcast.63, bf16[1024,1024]{1,0:T(8,128)(2,1)S(1)} %bitcast.65), kind=kOutput, calls=%fused_computation.18 | convolution fusion | flops 6470696960 | bytes 17039360 | tf_op jit(solution)/shard_map/dot_general | solution.py:22
  28.0 0.4 multiply_reduce_fusion.3
  28.4 0.6 copy-done.23
  29.1 0.7 pad_maximum_fusion.4
  29.9 0.5 exp.20
  30.4 80.4 %psum.14 = f32[100]{0:T(128)S(1)} all-reduce(f32[100]{0:T(128)} %convert_reduce_fusion.1), channel_id=1, replica_groups=mesh['blk'=16,'dp'=16] {'blk','dp'}, use_global_device_ids=true, to_apply=%region_4.0 | all-reduce | flops 100 | bytes 800 | tf_op jit(solution)/shard_map/psum | solution.py:92
  110.8 0.5 maximum_divide_fusion
  111.4 1.2 convert_reduce_fusion
  112.5 0.9 select_reduce_fusion.4
  113.4 5.5 %fusion.32 = (f32[1024]{0:T(1024)S(1)}, f32[1024]{0:T(1024)}, f32[1024,1024]{1,0:T(8,128)}) fusion(f32[1024]{0:T(1024)S(1)} %get-tuple-element.39, bf16[1024,1152]{1,0:T(8,128)(2,1)} %all-gather.2.cloned.1.call-done, f32[1024]{0:T(1024)S(1)} %get-tuple-element.40), kind=kOutput, calls=%fused_computation.86 | convolution fusion | flops 1077934080 | bytes 6307840 | tf_op jit(solution)/shard_map/dot_general | solution.py:104
  118.9 21.2 %gather_fusion = f32[1024]{0:T(1024)} fusion(f32[1024,1024]{1,0:T(8,128)} %get-tuple-element.54, s32[1024]{0:T(1024)S(1)} %bitcast.59), kind=kCustom, calls=%fused_computation | custom fusion | bytes 16384 | tf_op jit(solution)/shard_map/jit(diagonal)/cond/branch_0_fun/gather | solution.py:113
  140.1 3.9 exponential_reduce_fusion.1
  144.0 0.7 multiply_subtract_fusion
  144.7 3.8 multiply_reduce_fusion
  148.6 2.4 multiply_reduce_fusion.2
  151.0 0.5 convolution_multiply_fusion
  151.5 1.6 convolution_convert_fusion.1
  153.0 2.8 fusion.6
  155.9 10.7 %convolution_convert_fusion = bf16[3072,1024]{1,0:T(8,128)(2,1)} fusion(bf16[1024,1024]{1,0:T(8,128)(2,1)S(1)} %fusion.6, bf16[1024,1024]{1,0:T(8,128)(2,1)S(1)} %bitcast.68, bf16[1024,1024]{1,0:T(8,128)(2,1)S(1)} %bitcast.64, bf16[1024,1024]{1,0:T(8,128)(2,1)S(1)} %bitcast.66), kind=kOutput, calls=%fused_computation.7 | convolution fusion | flops 6464471040 | bytes 14680064 | tf_op jit(solution)/shard_map/dot_general | solution.py:55
  166.5 8.8 %copy.30 = bf16[3072,1024]{0,1:T(8,128)(2,1)} copy(bf16[3072,1024]{1,0:T(8,128)(2,1)} %convolution_convert_fusion) | data formatting | bytes 12582912 | tf_op jit(solution)/shard_map/convert_element_type | solution.py:64
  175.3 0.5 copy.32
  175.8 1.3 reshape.106
  177.2 3.5 copy.33
  180.7 6.0 %reshape.107 = bf16[16,16,2048]{2,1,0:T(8,128)(2,1)S(1)} reshape(bf16[16,16,64,32]{3,2,1,0:T(8,128)(2,1)} %copy.33) | data formatting | bytes 2097152 | tf_op jit(solution)/shard_map/reshape | solution.py:67
  186.7 14.6 %reshape.104 = bf16[16,192,16,64]{1,0,3,2:T(8,128)(2,1)} reshape(bf16[3072,1024]{0,1:T(8,128)(2,1)} %copy.30) | data formatting | bytes 12582912 | tf_op jit(solution)/shard_map/reshape | solution.py:65
  201.3 16.6 %copy.31 = bf16[16,16,192,64]{3,2,1,0:T(8,128)(2,1)} copy(bf16[16,16,192,64]{2,1,3,0:T(8,128)(2,1)} %bitcast.60) | data formatting | bytes 12582912 | tf_op jit(solution)/shard_map/transpose | solution.py:66
  217.9 17.0 %reshape.105 = bf16[16,16,12288]{2,1,0:T(8,128)(2,1)} reshape(bf16[16,16,192,64]{3,2,1,0:T(8,128)(2,1)} %copy.31) | data formatting | bytes 12582912 | tf_op jit(solution)/shard_map/reshape | solution.py:67
  235.1 6.5 %pad_maximum_fusion = bf16[16,16,14336]{2,1,0:T(8,128)(2,1)} fusion(bf16[16,16,2048]{2,1,0:T(8,128)(2,1)S(1)} %reshape.107, bf16[16,16,12288]{2,1,0:T(8,128)(2,1)} %reshape.105), kind=kLoop, calls=%fused_computation.1 | loop fusion | flops 14680064 | bytes 14680064 | tf_op jit(solution)/shard_map/concatenate | solution.py:143
  241.8 0.6 copy-done.32
  242.3 0.6 dynamic-slice
  242.9 30.2 %psum.15 = f32[2,100]{1,0:T(2,128)S(1)} all-reduce(f32[2,100]{1,0:T(2,128)S(1)} %pad_maximum_fusion.5), channel_id=1, replica_groups=mesh['blk'=16,'dp'=16] {'dp'}, use_global_device_ids=true, to_apply=%region_16.17 | all-reduce | flops 200 | bytes 1600 | tf_op jit(solution)/shard_map/psum | solution.py:150
  273.1 0.5 broadcast_subtract_fusion
  273.6 1.9 multiply_reduce_fusion.1
  275.5 64.4 %reduce-scatter.2.cloned.1.call-done = bf16[1,16,14336]{2,1,0:T(8,128)(2,1)} async-done(((bf16[16,16,14336]{2,1,0:T(8,128)(2,1)}), bf16[1,16,14336]{2,1,0:T(8,128)(2,1)}) %reduce-scatter.2.cloned.1.call-update) | async-done | bytes 458768 | tf_op jit(solution)/shard_map/reduce_scatter | solution.py:148
  339.9 0.6 add_reduce_fusion
  340.5 0.5 slice_bitcast_fusion
  341.1 0.7 divide_bitcast_fusion
  341.8 137.2 %all-reduce.5.cloned.1.call-done = bf16[16,14336]{1,0:T(8,128)(2,1)} async-done(((bf16[16,14336]{1,0:T(8,128)(2,1)}), bf16[16,14336]{1,0:T(8,128)(2,1)}) %all-reduce.5.cloned.1.call-update) | async-done | bytes 458768
  479.0 1.5 fusion.22
  480.6 0.7 copy.35
  481.3 1.7 fusion.21
  483.1 0.7 copy.34
  (80 shorter events, 1.5 us)
Async XLA Ops:
  7.2 20.8 %copy-start = (bf16[1024,512]{1,0:T(8,128)(2,1)S(1)}, bf16[1024,512]{1,0:T(8,128)(2,1)}, u32[]{:S(2)}) copy-start(bf16[1024,512]{1,0:T(8,128)(2,1)} %param.10) | copy-start | bytes 3145732
  7.2 104.2 %all-gather.2.cloned.1.call-start = ((), (), s32[]{:S(2)}) async-start(), calls=%async_computation.1 | async-start | bytes 2506752 | tf_op jit(solution)/shard_map/all_gather | solution.py:91
  10.2 18.2 %copy-start.21 = (f32[64]{0:T(128)}, f32[64]{0:T(128)S(1)}, u32[]{:S(2)}) copy-start(f32[64]{0:T(128)S(1)} %add_sqrt_fusion) | copy-start | bytes 772
  13.5 1.6 copy-start.3
  13.5 4.9 %copy-start.30 = (bf16[3072,1024]{1,0:T(8,128)(2,1)S(1)}, bf16[3072,1024]{1,0:T(8,128)(2,1)}, u32[]{:S(2)}) copy-start(bf16[3072,1024]{1,0:T(8,128)(2,1)} %param.9) | copy-start | bytes 18874372
  14.4 13.6 %copy-start.6 = (bf16[64,16,1024]{2,1,0:T(8,128)(2,1)}, bf16[64,16,1024]{2,1,0:T(8,128)(2,1)S(1)}, u32[]{:S(2)}) copy-start(bf16[64,16,1024]{2,1,0:T(8,128)(2,1)S(1)} %concatenate.26) | copy-start | bytes 6291460
  14.8 13.2 %copy-start.8 = (bf16[64,16,1024]{2,1,0:T(8,128)(2,1)}, bf16[64,16,1024]{2,1,0:T(8,128)(2,1)S(1)}, u32[]{:S(2)}) copy-start(bf16[64,16,1024]{2,1,0:T(8,128)(2,1)S(1)} %concatenate.29) | copy-start | bytes 6291460
  18.4 10.5 %copy-start.11 = (bf16[1,64,512]{2,1,0:T(8,128)(2,1)S(1)}, bf16[1,64,512]{2,1,0:T(8,128)(2,1)}, u32[]{:S(2)}) copy-start(bf16[1,64,512]{2,1,0:T(8,128)(2,1)} %param.11) | copy-start | bytes 196612
  18.4 11.5 %copy-start.31 = (f32[100]{0:T(128)S(1)}, f32[100]{0:T(128)}, u32[]{:S(2)}) copy-start(f32[100]{0:T(128)} %param.13) | copy-start | bytes 1204
  18.4 92.4 %copy-start.26 = (f32[100]{0:T(128)S(1)}, f32[100]{0:T(128)}, u32[]{:S(2)}) copy-start(f32[100]{0:T(128)} %param.15) | copy-start | bytes 1204
  18.4 94.1 %copy-start.25 = (f32[100]{0:T(128)S(1)}, f32[100]{0:T(128)}, u32[]{:S(2)}) copy-start(f32[100]{0:T(128)} %param.14) | copy-start | bytes 1204
  28.4 0.6 copy-start.23
  29.8 310.1 %reduce-scatter.2.cloned.1.call-start = ((), (), s32[]{:S(2)}) async-start(), calls=%async_computation.2 | async-start | bytes 7798784 | tf_op jit(solution)/shard_map/reduce_scatter | solution.py:148
  110.8 0.5 copy-start.28
  113.4 5.5 %copy-start.14 = (f32[1024]{0:T(1024)}, f32[1024]{0:T(1024)S(1)}, u32[]{:S(2)}) copy-start(f32[1024]{0:T(1024)S(1)} %get-tuple-element.39) | copy-start | bytes 12292
  113.4 5.5 %copy-start.16 = (f32[1024]{0:T(1024)}, f32[1024]{0:T(1024)S(1)}, u32[]{:S(2)}) copy-start(f32[1024]{0:T(1024)S(1)} %get-tuple-element.40) | copy-start | bytes 12292
  118.9 25.0 %copy-start.18 = (f32[1024]{0:T(1024)}, f32[1024]{0:T(1024)S(1)}, u32[]{:S(2)}) copy-start(f32[1024]{0:T(1024)S(1)} %get-tuple-element.34) | copy-start | bytes 12292
  140.1 3.9 copy-start.19
  140.1 3.9 copy-start.20
  140.1 4.6 copy-start.2
  140.1 4.6 copy-start.15
  140.1 4.6 copy-start.17
  144.0 4.6 copy-start.24
  144.7 8.3 %copy-start.4 = (f32[1024,1024]{1,0:T(8,128)S(1)}, f32[1024,1024]{1,0:T(8,128)}, u32[]{:S(2)}) copy-start(f32[1024,1024]{1,0:T(8,128)} %get-tuple-element.51) | copy-start | bytes 12582916
  148.6 4.4 copy-start.10
  151.4 4.4 copy-start.7
  151.4 4.4 copy-start.9
  166.5 8.8 %copy-start.5 = (bf16[1024,512]{1,0:T(8,128)(2,1)S(1)}, bf16[1024,512]{1,0:T(8,128)(2,1)}, u32[]{:S(2)}) copy-start(bf16[1024,512]{1,0:T(8,128)(2,1)} %convolution_convert_fusion.1) | copy-start | bytes 3145732
  217.9 17.0 %copy-start.13 = (f32[1024]{0:T(1024)S(1)}, f32[1024]{0:T(1024)}, u32[]{:S(2)}) copy-start(f32[1024]{0:T(1024)} %get-tuple-element.46) | copy-start | bytes 12292
  241.7 0.7 copy-start.32
  241.7 31.4 %copy-start.27 = (f32[100]{0:T(128)S(1)}, f32[100]{0:T(128)}, u32[]{:S(2)}) copy-start(f32[100]{0:T(128)} %param.15) | copy-start | bytes 1204
  241.7 31.4 %copy-start.29 = (f32[100]{0:T(128)S(1)}, f32[100]{0:T(128)}, u32[]{:S(2)}) copy-start(f32[100]{0:T(128)} %copy-done.28) | copy-start | bytes 1204
  241.7 31.9 %copy-start.12 = (bf16[1,64,512]{2,1,0:T(8,128)(2,1)S(1)}, bf16[1,64,512]{2,1,0:T(8,128)(2,1)}, u32[]{:S(2)}) copy-start(bf16[1,64,512]{2,1,0:T(8,128)(2,1)} %param.11) | copy-start | bytes 196612
  241.7 31.9 %copy-start.22 = (f32[64]{0:T(128)S(1)}, f32[64]{0:T(128)}, u32[]{:S(2)}) copy-start(f32[64]{0:T(128)} %copy-done.21) | copy-start | bytes 772
  241.7 242.1 %copy-start.1 = (bf16[1024,512]{1,0:T(8,128)(2,1)S(1)}, bf16[1024,512]{1,0:T(8,128)(2,1)}, u32[]{:S(2)}) copy-start(bf16[1024,512]{1,0:T(8,128)(2,1)} %param.10) | copy-start | bytes 3145732
  241.7 237.3 %all-reduce.5.cloned.1.call-start = ((), (), s32[]{:S(2)}) async-start(), calls=%async_computation.3 | async-start | bytes 917504
Sparse Core Ops, SparseCore 0:
  30.0 77.0 all-gather.1
  241.8 98.0 reduce-scatter.1
  342.6 136.4 all-reduce.4

commit v2 on v1

--- a/solution.py
+++ b/solution.py
@@ -39,8 +39,8 @@
     steps_count = preact.shape[0] // clips
     radial = jnp.sum(audio_unit * grad_audio, axis=-1, keepdims=True)
     grad_embed = ((grad_audio - audio_unit * radial) / audio_len).astype(jnp.bfloat16)
-    proj_term = lax.dot_general(
-        pooled, grad_embed, (((0,), (0,)), ((), ())), preferred_element_type=jnp.float32
+    proj_term_t = lax.dot_general(
+        grad_embed, pooled, (((0,), (0,)), ((), ())), preferred_element_type=jnp.float32
     )
     grad_pooled = (
         lax.dot_general(
@@ -52,20 +52,31 @@
         grad_pooled[:, None, :], (clips, steps_count, grad_pooled.shape[1])
     ).reshape(clips * steps_count, -1)
     grad_pre = jax.vjp(jax.nn.gelu, preact)[1](grad_act)[0].astype(jnp.bfloat16)
-    conv_term = lax.dot_general(
-        stacked, grad_pre, (((0,), (0,)), ((), ())), preferred_element_type=jnp.float32
+    conv_term_t = lax.dot_general(
+        grad_pre, stacked, (((0,), (0,)), ((), ())), preferred_element_type=jnp.float32
     )
-    return (conv_term, proj_term)
+    return (conv_term_t, proj_term_t)
 
 
-def blocks_for_scatter(term, n_blk, n_dp):
-    rows, cols = term.shape
-    return (
-        term.astype(jnp.bfloat16)
-        .reshape(n_blk, rows // n_blk, n_dp, cols // n_dp)
-        .transpose(2, 0, 1, 3)
-        .reshape(n_dp, n_blk, (rows // n_blk) * (cols // n_dp))
+def scatter_buffer(conv_term_t, proj_term_t, n_blk, n_dp):
+    width = conv_term_t.shape[1]
+    conv_part = conv_term_t.astype(jnp.bfloat16).reshape(n_dp, -1, width)
+    p_cols, p_rows = proj_term_t.shape
+    per_block = (p_cols // n_dp) * (p_rows // n_blk)
+    seg = width // n_blk
+    pad_rows = -(-per_block // seg)
+    pad_rows = -(-pad_rows // 16) * 16
+    proj_part = (
+        proj_term_t.astype(jnp.bfloat16)
+        .reshape(n_dp, p_cols // n_dp, n_blk, p_rows // n_blk)
+        .transpose(0, 2, 1, 3)
+        .reshape(n_dp, n_blk, per_block)
     )
+    proj_part = jnp.pad(proj_part, ((0, 0), (0, 0), (0, pad_rows * seg - per_block)))
+    proj_part = (
+        proj_part.reshape(n_dp, n_blk, pad_rows, seg).transpose(0, 2, 1, 3).reshape(n_dp, pad_rows, width)
+    )
+    return jnp.concatenate([conv_part, proj_part], axis=1), per_block
 
 
 def local(
@@ -110,10 +121,10 @@
     row_lse = row_max + jnp.log(jnp.sum(jnp.exp(logits - row_max[:, None]), axis=1))
     col_max = jnp.max(logits, axis=0)
     col_lse = col_max + jnp.log(jnp.sum(jnp.exp(logits - col_max[None, :]), axis=0))
-    positive = jnp.diagonal(logits)
-    pair_loss = 0.5 * (row_lse + col_lse) - positive
     index = jnp.arange(logits.shape[0], dtype=jnp.int32)
     on_diagonal = index[:, None] == index[None, :]
+    positive = jnp.sum(jnp.where(on_diagonal, logits, 0.0), axis=1)
+    pair_loss = 0.5 * (row_lse + col_lse) - positive
     score_grad = 0.5 * (
         pair_weight[:, None] * jnp.exp(logits - row_lse[:, None])
         + pair_weight[None, :] * jnp.exp(logits - col_lse[None, :])
@@ -137,25 +148,21 @@
             jnp.sum(all_onehot * scale_terms[:, None], axis=0),
         ]
     )
-    conv_term, proj_term = encode_back(
+    conv_term_t, proj_term_t = encode_back(
         stacked, preact, pooled, audio_unit, audio_len, grad_audio, proj_weight
     )
-    buf = jnp.concatenate(
-        [blocks_for_scatter(conv_term, n_blk, n_dp), blocks_for_scatter(proj_term, n_blk, n_dp)],
-        axis=2,
-    )
+    buf, per_block = scatter_buffer(conv_term_t, proj_term_t, n_blk, n_dp)
     buf, batch_sums = lax.optimization_barrier((buf, batch_sums))
     stage = lax.psum_scatter(buf, "dp", scatter_dimension=0, tiled=True)
-    stage = lax.psum_scatter(stage.reshape(n_blk, -1), "blk", scatter_dimension=0, tiled=True)
+    stage = lax.psum_scatter(stage[0], "blk", scatter_dimension=1, tiled=True)
     loss_sum, scale_grad = lax.psum(batch_sums, "dp")
-    conv_rows = conv_term.shape[0] // n_blk
-    conv_cols = conv_term.shape[1] // n_dp
-    conv_size = conv_rows * conv_cols
-    conv_grad = stage[0, :conv_size].reshape(conv_rows, conv_cols).astype(jnp.float32)
+    conv_cols = conv_term_t.shape[0] // n_dp
+    conv_grad = stage[:conv_cols].T.astype(jnp.float32)
     proj_grad = (
-        stage[0, conv_size:]
-        .reshape(proj_term.shape[0] // n_blk, proj_term.shape[1] // n_dp)
-        .astype(jnp.float32)
+        stage[conv_cols:]
+        .reshape(-1)[:per_block]
+        .reshape(proj_term_t.shape[0] // n_dp, proj_term_t.shape[1] // n_blk)
+        .T.astype(jnp.float32)
     )
     var_weight = jnp.exp(-log_var)
     lang_mean = loss_sum / jnp.maximum(counts, 1.0)

time: 493 us -> 349 us (0.71)
  local copies, waits for them, and re-layouts: 102 us -> 33.3 us
  waiting for transfers between devices: 202 us -> 137 us
  other arithmetic: 29.3 us -> 23.5 us
    unnamed x4, waiting for transfers between devices: 137 us -> 67.1 us
    reshape x4 -> x5, local copies, waits for them, and re-layouts: 39 us -> 15.6 us  [the longest x3 8.19 us: scatter_buffer(): proj_part = proj_term_t.astype(jnp.bfloat16).reshape(n_dp, p_cols // n_dp...]
    gather x1 -> x0, local copies, waits for them, and re-layouts: 21.2 us -> none  [local(): positive = jnp.diagonal(logits)]
    transpose x2 -> x1, local copies, waits for them, and re-layouts: 20.1 us -> 2.19 us  [scatter_buffer(): proj_part.reshape(n_dp, n_blk, pad_rows, seg).transpose(0, 2, 1, 3)]
    convert_element_type x4 -> x0, local copies, waits for them, and re-layouts: 9.43 us -> none  [the longest x2 9.28 us: blocks_for_scatter(): term.astype(jnp.bfloat16).reshape(n_blk, rows // n_blk, n_dp, cols // n_dp)]
    reduce_scatter x1, waiting for transfers between devices: 64.4 us -> 70.4 us  [local(): stage = lax.psum_scatter(buf, 'dp', scatter_dimension=0, tiled=True)]
  transfers between devices with their start and end apart: 3 -> 3, of which waited for: 2 -> 2; matrix products, arithmetic and copies ran while one was open for 1% -> 2% of each run, Pallas kernels for 0% -> 0%
where the time goes in v2:
time: 349 us; the launch traced here: 348 us
  waiting for transfers between devices  137 us (39%)
  blocking collectives  111 us (32%)
  local copies, waits for them, and re-layouts  33.3 us (10%)
  matrix products  28.5 us (8%)
  other arithmetic  23.5 us (7%)
  between operations  14.1 us (4%)
    psum x1, blocking collectives, local(): counts = lax.psum(local_counts, ('blk', 'dp'))  80.3 us
    reduce_scatter x1, waiting for transfers between devices, local(): stage = lax.psum_scatter(buf, 'dp', scatter_dimension=0, tiled=True)  70.4 us
    unnamed x4, waiting for transfers between devices  67.1 us
    psum x1, blocking collectives, local(): loss_sum, scale_grad = lax.psum(batch_sums, 'dp')  30.5 us
    dot_general x1, matrix products, encode_back(): lax.dot_general(grad_pre, stacked, (((0,), (0,)), ((), ())), preferred_el...  9.45 us
    dot_general x1, matrix products, encode(): preact = jnp.dot(stacked, conv_weight, preferred_element_type=jnp.float32)  9.37 us
    reshape x3, local copies, waits for them, and re-layouts, scatter_buffer(): proj_part = proj_term_t.astype(jnp.bfloat16).reshape(n_dp, p_cols // n_dp...  8.19 us
    reshape x2, local copies, waits for them, and re-layouts, scatter_buffer(): proj_part.reshape(n_dp, n_blk, pad_rows, seg).transpose(0, 2, 1, 3)  7.38 us
  transfers between devices with their start and end apart: 3, of which 2 were waited for; matrix products, arithmetic and copies ran while one was open for 2% of the time, Pallas kernels for 0%

profile of v2, /device:TPU:8, one launch (start us, length us, event | category | flops | bytes accessed | tf_op | source)
XLA Modules:
  0.0 347.8 jit_solution(2965290226560186830)
XLA Ops:
  7.2 3.3 fusion.32
  10.6 0.9 concatenate.22
  11.5 0.4 concatenate.25
  11.9 0.3 copy-done.1
  12.2 3.3 copy-done.16
  15.5 9.4 %bitcast_reduce_fusion = (f32[64,1024]{1,0:T(8,128)S(1)}, f32[1024,1024]{1,0:T(8,128)}) fusion(bf16[3072,1024]{1,0:T(8,128)(2,1)S(1)} %copy-done.16, bf16[1024,1024]{1,0:T(8,128)(2,1)S(1)} %bitcast.72, bf16[1024,1024]{1,0:T(8,128)(2,1)S(1)} %bitcast.65, bf16[1024,1024]{1,0:T(8,128)(2,1)S(1)} %bitcast.70), kind=kOutput, calls=%fused_computation.17 | convolution fusion | flops 6470696960 | bytes 17039360 | tf_op jit(solution)/shard_map/dot_general | solution.py:22
  24.9 0.4 multiply_reduce_fusion.3
  25.3 0.1 fusion.18
  25.5 0.6 convert_reduce_fusion.1
  26.1 0.1 fusion.28
  26.2 0.1 broadcast_in_dim.13
  26.3 0.7 pad_maximum_fusion.4
  27.0 1.2 exp.20
  28.2 80.3 %psum.14 = f32[100]{0:T(128)S(1)} all-reduce(f32[100]{0:T(128)} %convert_reduce_fusion.1), channel_id=1, replica_groups=mesh['blk'=16,'dp'=16] {'blk','dp'}, use_global_device_ids=true, to_apply=%region_4.0 | all-reduce | flops 100 | bytes 800 | tf_op jit(solution)/shard_map/psum | solution.py:103
  108.5 1.2 maximum_divide_fusion
  109.7 1.2 convert_reduce_fusion
  110.9 0.9 select_reduce_fusion.5
  111.7 3.0 fusion.30
  114.8 2.6 select_reduce_fusion
  117.4 3.2 multiply_reduce_fusion
  120.7 2.4 multiply_reduce_fusion.2
  123.0 0.5 convolution_multiply_fusion
  123.5 1.6 convolution_convert_fusion.1
  125.1 2.8 fusion.6
  128.0 9.5 %convolution_convert_fusion = bf16[1024,3072]{1,0:T(8,128)(2,1)} fusion(bf16[1024,1024]{1,0:T(8,128)(2,1)S(1)} %fusion.6, bf16[1024,1024]{1,0:T(8,128)(2,1)S(1)} %bitcast.73, bf16[1024,1024]{1,0:T(8,128)(2,1)S(1)} %bitcast.66, bf16[1024,1024]{1,0:T(8,128)(2,1)S(1)} %bitcast.71), kind=kOutput, calls=%fused_computation.6 | convolution fusion | flops 6464471040 | bytes 14680064 | tf_op jit(solution)/shard_map/dot_general | solution.py:55
  137.4 2.9 reshape.105
  140.4 1.9 copy.32
  142.3 3.4 reshape.106
  145.6 1.3 pad.6
  147.0 3.7 %reshape.107 = bf16[16,16,16,192]{3,2,1,0:T(8,128)(2,1)S(1)} reshape(bf16[16,16,3072]{2,1,0:T(8,128)(2,1)} %pad.6) | data formatting | bytes 3145728 | tf_op jit(solution)/shard_map/reshape | solution.py:77
  150.7 2.2 copy.25
  152.9 3.7 %reshape.108 = bf16[16,16,3072]{2,1,0:T(8,128)(2,1)S(1)} reshape(bf16[16,16,16,192]{3,2,1,0:T(8,128)(2,1)} %copy.25) | data formatting | bytes 3145728 | tf_op jit(solution)/shard_map/reshape | solution.py:77
  156.5 0.2 select_reduce_fusion.2
  156.7 6.8 %pad_maximum_fusion = bf16[16,80,3072]{2,1,0:T(8,128)(2,1)} fusion(bf16[16,16,3072]{2,1,0:T(8,128)(2,1)S(1)} %reshape.108, bf16[16,64,3072]{2,1,0:T(8,128)(2,1)} %bitcast.68), kind=kLoop, calls=%fused_computation | loop fusion | flops 15728640 | bytes 15728640 | tf_op jit(solution)/shard_map/concatenate | solution.py:79
  163.6 30.5 %psum.15 = f32[2,100]{1,0:T(2,128)S(1)} all-reduce(f32[2,100]{1,0:T(2,128)S(1)} %pad_maximum_fusion.5), channel_id=1, replica_groups=mesh['blk'=16,'dp'=16] {'dp'}, use_global_device_ids=true, to_apply=%region_17.18 | all-reduce | flops 200 | bytes 1600 | tf_op jit(solution)/shard_map/psum | solution.py:158
  194.1 70.4 %reduce-scatter.5.cloned.1.call-done = bf16[1,80,3072]{2,1,0:T(8,128)(2,1)} async-done(((bf16[16,80,3072]{2,1,0:T(8,128)(2,1)}), bf16[1,80,3072]{2,1,0:T(8,128)(2,1)}) %reduce-scatter.5.cloned.1.call-update) | async-done | bytes 491536 | tf_op jit(solution)/shard_map/reduce_scatter | solution.py:156
  264.5 2.2 copy.27
  266.8 0.5 broadcast_subtract_fusion
  267.3 0.6 add_reduce_fusion
  267.9 0.5 slice_bitcast_fusion
  268.4 1.9 multiply_reduce_fusion.1
  270.3 0.8 divide_bitcast_fusion
  271.0 67.0 %reduce-scatter.7.cloned.1.call-done = bf16[192,80]{1,0:T(8,128)(2,1)} async-done(((bf16[3072,80]{1,0:T(8,128)(2,1)}), bf16[192,80]{1,0:T(8,128)(2,1)}) %reduce-scatter.7.cloned.1.call-update) | async-done | bytes 30736
  338.0 0.9 slice.42
  338.9 0.9 copy.29
  339.8 0.6 convert_bitcast_fusion
  340.5 0.1 slice.34
  340.6 0.6 convert_bitcast_fusion.1
  (47 shorter events, 0.4 us)
Async XLA Ops:
  7.2 17.7 %copy-start = (bf16[1024,512]{1,0:T(8,128)(2,1)S(1)}, bf16[1024,512]{1,0:T(8,128)(2,1)}, u32[]{:S(2)}) copy-start(bf16[1024,512]{1,0:T(8,128)(2,1)} %param.10) | copy-start | bytes 3145732
  7.2 102.5 %all-gather.2.cloned.1.call-start = ((), (), s32[]{:S(2)}) async-start(), calls=%async_computation.2 | async-start | bytes 2506752 | tf_op jit(solution)/shard_map/all_gather | solution.py:102
  10.6 1.6 copy-start.1
  10.6 4.9 %copy-start.16 = (bf16[3072,1024]{1,0:T(8,128)(2,1)S(1)}, bf16[3072,1024]{1,0:T(8,128)(2,1)}, u32[]{:S(2)}) copy-start(bf16[3072,1024]{1,0:T(8,128)(2,1)} %param.9) | copy-start | bytes 18874372
  11.5 13.4 %copy-start.3 = (bf16[64,16,1024]{2,1,0:T(8,128)(2,1)}, bf16[64,16,1024]{2,1,0:T(8,128)(2,1)S(1)}, u32[]{:S(2)}) copy-start(bf16[64,16,1024]{2,1,0:T(8,128)(2,1)S(1)} %concatenate.22) | copy-start | bytes 6291460
  11.9 13.0 %copy-start.5 = (bf16[64,16,1024]{2,1,0:T(8,128)(2,1)}, bf16[64,16,1024]{2,1,0:T(8,128)(2,1)S(1)}, u32[]{:S(2)}) copy-start(bf16[64,16,1024]{2,1,0:T(8,128)(2,1)S(1)} %concatenate.25) | copy-start | bytes 6291460
  15.5 9.8 %copy-start.8 = (bf16[1,64,512]{2,1,0:T(8,128)(2,1)S(1)}, bf16[1,64,512]{2,1,0:T(8,128)(2,1)}, u32[]{:S(2)}) copy-start(bf16[1,64,512]{2,1,0:T(8,128)(2,1)} %param.11) | copy-start | bytes 196612
  15.5 9.9 %copy-start.17 = (s32[1,64]{1,0:T(1,128)S(1)}, s32[1,64]{1,0:T(1,128)}, u32[]{:S(2)}) copy-start(s32[1,64]{1,0:T(1,128)} %param.12) | copy-start | bytes 772
  15.5 95.3 %copy-start.12 = (f32[100]{0:T(128)S(1)}, f32[100]{0:T(128)}, u32[]{:S(2)}) copy-start(f32[100]{0:T(128)} %param.14) | copy-start | bytes 1204
  25.3 84.4 %copy-start.10 = (f32[64]{0:T(128)}, f32[64]{0:T(128)S(1)}, u32[]{:S(2)}) copy-start(f32[64]{0:T(128)S(1)} %add_sqrt_fusion.1) | copy-start | bytes 772
  27.0 237.6 %reduce-scatter.5.cloned.1.call-start = ((), (), s32[]{:S(2)}) async-start(), calls=%async_computation.3 | async-start | bytes 8355840 | tf_op jit(solution)/shard_map/reduce_scatter | solution.py:156
  108.5 6.2 %copy-start.14 = (f32[100]{0:T(128)}, f32[100]{0:T(128)S(1)}, u32[]{:S(2)}) copy-start(f32[100]{0:T(128)S(1)} %psum.14) | copy-start | bytes 1204
  117.4 3.3 copy-start.11
  117.4 7.7 %copy-start.2 = (f32[1024,1024]{1,0:T(8,128)S(1)}, f32[1024,1024]{1,0:T(8,128)}, u32[]{:S(2)}) copy-start(f32[1024,1024]{1,0:T(8,128)} %get-tuple-element.34) | copy-start | bytes 12582916
  120.6 4.5 %copy-start.7 = (bf16[1024,1024]{1,0:T(8,128)(2,1)}, bf16[1024,1024]{1,0:T(8,128)(2,1)S(1)}, u32[]{:S(2)}) copy-start(bf16[1024,1024]{1,0:T(8,128)(2,1)S(1)} %get-tuple-element.30) | copy-start | bytes 6291460
  123.5 4.4 %copy-start.4 = (bf16[64,16,1024]{2,1,0:T(8,128)(2,1)S(1)}, bf16[64,16,1024]{2,1,0:T(8,128)(2,1)}, u32[]{:S(2)}) copy-start(bf16[64,16,1024]{2,1,0:T(8,128)(2,1)} %copy-done.3) | copy-start | bytes 6291460
  123.5 4.4 %copy-start.6 = (bf16[64,16,1024]{2,1,0:T(8,128)(2,1)S(1)}, bf16[64,16,1024]{2,1,0:T(8,128)(2,1)}, u32[]{:S(2)}) copy-start(bf16[64,16,1024]{2,1,0:T(8,128)(2,1)} %copy-done.5) | copy-start | bytes 6291460
  163.6 103.2 %copy-start.13 = (f32[100]{0:T(128)S(1)}, f32[100]{0:T(128)}, u32[]{:S(2)}) copy-start(f32[100]{0:T(128)} %param.15) | copy-start | bytes 1204
  163.6 103.2 %copy-start.15 = (f32[100]{0:T(128)S(1)}, f32[100]{0:T(128)}, u32[]{:S(2)}) copy-start(f32[100]{0:T(128)} %copy-done.14) | copy-start | bytes 1204
  163.6 104.8 %copy-start.9 = (bf16[1,64,512]{2,1,0:T(8,128)(2,1)S(1)}, bf16[1,64,512]{2,1,0:T(8,128)(2,1)}, u32[]{:S(2)}) copy-start(bf16[1,64,512]{2,1,0:T(8,128)(2,1)} %param.11) | copy-start | bytes 196612
  163.6 174.5 %reduce-scatter.7.cloned.1.call-start = ((), (), s32[]{:S(2)}) async-start(), calls=%async_computation.4 | async-start | bytes 835584
Sparse Core Ops, SparseCore 0:
  27.1 77.4 all-gather.1
  163.7 100.7 reduce-scatter.4
  267.0 70.9 reduce-scatter.6

commit v3 on v1

--- a/solution.py
+++ b/solution.py
@@ -34,13 +34,19 @@
     return (text_float / text_len, text_len)
 
 
-def encode_back(stacked, preact, pooled, audio_unit, audio_len, grad_audio, proj_weight):
+def encode_back(stacked, preact, pooled, audio_unit, audio_len, grad_audio, proj_weight, n_dp):
     clips = pooled.shape[0]
     steps_count = preact.shape[0] // clips
     radial = jnp.sum(audio_unit * grad_audio, axis=-1, keepdims=True)
     grad_embed = ((grad_audio - audio_unit * radial) / audio_len).astype(jnp.bfloat16)
+    emb = grad_embed.shape[1]
+    width = preact.shape[1]
+    padded = jnp.pad(
+        grad_embed.reshape(clips, n_dp, emb // n_dp),
+        ((0, 0), (0, 0), (0, (width - emb) // n_dp)),
+    ).reshape(clips, width)
     proj_term = lax.dot_general(
-        pooled, grad_embed, (((0,), (0,)), ((), ())), preferred_element_type=jnp.float32
+        pooled, padded, (((0,), (0,)), ((), ())), preferred_element_type=jnp.float32
     )
     grad_pooled = (
         lax.dot_general(
@@ -56,16 +62,6 @@
         stacked, grad_pre, (((0,), (0,)), ((), ())), preferred_element_type=jnp.float32
     )
     return (conv_term, proj_term)
-
-
-def blocks_for_scatter(term, n_blk, n_dp):
-    rows, cols = term.shape
-    return (
-        term.astype(jnp.bfloat16)
-        .reshape(n_blk, rows // n_blk, n_dp, cols // n_dp)
-        .transpose(2, 0, 1, 3)
-        .reshape(n_dp, n_blk, (rows // n_blk) * (cols // n_dp))
-    )
 
 
 def local(
@@ -110,10 +106,10 @@
     row_lse = row_max + jnp.log(jnp.sum(jnp.exp(logits - row_max[:, None]), axis=1))
     col_max = jnp.max(logits, axis=0)
     col_lse = col_max + jnp.log(jnp.sum(jnp.exp(logits - col_max[None, :]), axis=0))
-    positive = jnp.diagonal(logits)
-    pair_loss = 0.5 * (row_lse + col_lse) - positive
     index = jnp.arange(logits.shape[0], dtype=jnp.int32)
     on_diagonal = index[:, None] == index[None, :]
+    positive = jnp.sum(jnp.where(on_diagonal, logits, 0.0), axis=1)
+    pair_loss = 0.5 * (row_lse + col_lse) - positive
     score_grad = 0.5 * (
         pair_weight[:, None] * jnp.exp(logits - row_lse[:, None])
         + pair_weight[None, :] * jnp.exp(logits - col_lse[None, :])
@@ -138,25 +134,23 @@
         ]
     )
     conv_term, proj_term = encode_back(
-        stacked, preact, pooled, audio_unit, audio_len, grad_audio, proj_weight
+        stacked, preact, pooled, audio_unit, audio_len, grad_audio, proj_weight, n_dp
     )
+    conv_rows = conv_term.shape[0] // n_blk
+    proj_rows = proj_term.shape[0] // n_blk
     buf = jnp.concatenate(
-        [blocks_for_scatter(conv_term, n_blk, n_dp), blocks_for_scatter(proj_term, n_blk, n_dp)],
-        axis=2,
+        [
+            conv_term.astype(jnp.bfloat16).reshape(n_blk, conv_rows, -1),
+            proj_term.astype(jnp.bfloat16).reshape(n_blk, proj_rows, -1),
+        ],
+        axis=1,
     )
     buf, batch_sums = lax.optimization_barrier((buf, batch_sums))
-    stage = lax.psum_scatter(buf, "dp", scatter_dimension=0, tiled=True)
-    stage = lax.psum_scatter(stage.reshape(n_blk, -1), "blk", scatter_dimension=0, tiled=True)
+    stage = lax.psum_scatter(buf, "blk", scatter_dimension=0, tiled=True)
+    stage = lax.psum_scatter(stage[0], "dp", scatter_dimension=1, tiled=True)
     loss_sum, scale_grad = lax.psum(batch_sums, "dp")
-    conv_rows = conv_term.shape[0] // n_blk
-    conv_cols = conv_term.shape[1] // n_dp
-    conv_size = conv_rows * conv_cols
-    conv_grad = stage[0, :conv_size].reshape(conv_rows, conv_cols).astype(jnp.float32)
-    proj_grad = (
-        stage[0, conv_size:]
-        .reshape(proj_term.shape[0] // n_blk, proj_term.shape[1] // n_dp)
-        .astype(jnp.float32)
-    )
+    conv_grad = stage[:conv_rows].astype(jnp.float32)
+    proj_grad = stage[conv_rows:, : emb // n_dp].astype(jnp.float32)
     var_weight = jnp.exp(-log_var)
     lang_mean = loss_sum / jnp.maximum(counts, 1.0)
     loss = jnp.sum(var_weight * lang_mean + log_var)

time: 493 us -> 437 us (0.89)
  local copies, waits for them, and re-layouts: 102 us -> 26.5 us
  waiting for transfers between devices: 202 us -> 219 us
    reduce_scatter x1 -> x2, waiting for transfers between devices: 64.4 us -> 219 us  [the longest x1 145 us: local(): stage = lax.psum_scatter(buf, 'blk', scatter_dimension=0, tiled=True)]
    unnamed x4 -> x3, waiting for transfers between devices: 137 us -> 0.05 us
    reshape x4 -> x2, local copies, waits for them, and re-layouts: 39 us -> 14.2 us  [the longest x1 11 us: local(): conv_term.astype(jnp.bfloat16).reshape(n_blk, conv_rows, -1)]
    gather x1 -> x0, local copies, waits for them, and re-layouts: 21.2 us -> none  [local(): positive = jnp.diagonal(logits)]
    transpose x2 -> x0, local copies, waits for them, and re-layouts: 20.1 us -> none  [blocks_for_scatter(): return term.astype(jnp.bfloat16).reshape(n_blk, rows // n_blk, n_dp, cols...]
    convert_element_type x4 -> x1, local copies, waits for them, and re-layouts: 9.43 us -> 0.95 us  [encode_back(): ((grad_audio - audio_unit * radial) / audio_len).astype(jnp.bfloat16)]
    concatenate x2 -> x1, other arithmetic: 6.53 us -> 10.4 us  [local(): jnp.concatenate([conv_term.astype(jnp.bfloat16).reshape(n_blk, conv_rows,...]
  transfers between devices with their start and end apart: 3 -> 3, of which waited for: 2 -> 2; matrix products, arithmetic and copies ran while one was open for 1% -> 2% of each run, Pallas kernels for 0% -> 0%
where the time goes in v3:
time: 437 us; the launch traced here: 436 us
  waiting for transfers between devices  219 us (50%)
  blocking collectives  114 us (26%)
  other arithmetic  33.2 us (8%)
  matrix products  29.1 us (7%)
  local copies, waits for them, and re-layouts  26.5 us (6%)
  between operations  14 us (3%)
    reduce_scatter x1, waiting for transfers between devices, local(): stage = lax.psum_scatter(buf, 'blk', scatter_dimension=0, tiled=True)  145 us
    psum x1, blocking collectives, local(): counts = lax.psum(local_counts, ('blk', 'dp'))  80.1 us
    reduce_scatter x1, waiting for transfers between devices, local(): stage = lax.psum_scatter(stage[0], 'dp', scatter_dimension=1, tiled=True)  74.3 us
    psum x1, blocking collectives, local(): loss_sum, scale_grad = lax.psum(batch_sums, 'dp')  33.8 us
    reshape x1, local copies, waits for them, and re-layouts, local(): conv_term.astype(jnp.bfloat16).reshape(n_blk, conv_rows, -1)  11 us
    dot_general x1, matrix products, encode_back(): lax.dot_general(stacked, grad_pre, (((0,), (0,)), ((), ())), preferred_el...  10.5 us
    concatenate x1, other arithmetic, local(): jnp.concatenate([conv_term.astype(jnp.bfloat16).reshape(n_blk, conv_rows,...  10.4 us
    dot_general x1, matrix products, encode(): preact = jnp.dot(stacked, conv_weight, preferred_element_type=jnp.float32)  9.52 us
  transfers between devices with their start and end apart: 3, of which 2 were waited for; matrix products, arithmetic and copies ran while one was open for 2% of the time, Pallas kernels for 0%

profile of v3, /device:TPU:8, one launch (start us, length us, event | category | flops | bytes accessed | tf_op | source)
XLA Modules:
  0.0 436.3 jit_solution(15670300662268475790)
XLA Ops:
  7.2 0.0 all-gather.2.cloned.1.call-start
  7.2 0.7 bitcast_convert_fusion
  8.0 1.3 convert_reduce_fusion.1
  9.2 1.0 fusion.18
  10.2 3.3 fusion.32
  13.5 0.9 concatenate.22
  14.4 0.4 concatenate.25
  14.8 0.3 copy-done.1
  15.1 3.3 copy-done.15
  18.4 9.5 %bitcast_reduce_fusion = (f32[64,1024]{1,0:T(8,128)S(1)}, f32[1024,1024]{1,0:T(8,128)}) fusion(bf16[3072,1024]{1,0:T(8,128)(2,1)S(1)} %copy-done.15, bf16[1024,1024]{1,0:T(8,128)(2,1)S(1)} %bitcast.60, bf16[1024,1024]{1,0:T(8,128)(2,1)S(1)} %bitcast.55, bf16[1024,1024]{1,0:T(8,128)(2,1)S(1)} %bitcast.58), kind=kOutput, calls=%fused_computation.17 | convolution fusion | flops 6470696960 | bytes 17039360 | tf_op jit(solution)/shard_map/dot_general | solution.py:22
  28.0 0.4 multiply_reduce_fusion.3
  28.4 0.1 fusion.28
  28.5 0.1 broadcast_in_dim.13
  28.6 0.7 pad_maximum_fusion.4
  29.2 0.0 all-gather.2.cloned.1.call-update
  29.3 0.0 reduce-scatter.3.cloned.1.call-start
  29.3 1.2 exp.20
  30.5 80.1 %psum.14 = f32[100]{0:T(128)S(1)} all-reduce(f32[100]{0:T(128)} %convert_reduce_fusion.1), channel_id=1, replica_groups=mesh['blk'=16,'dp'=16] {'blk','dp'}, use_global_device_ids=true, to_apply=%region_4.0 | all-reduce | flops 100 | bytes 800 | tf_op jit(solution)/shard_map/psum | solution.py:88
  110.6 1.2 maximum_divide_fusion
  111.8 1.2 convert_reduce_fusion
  113.0 0.9 select_reduce_fusion.5
  113.8 3.0 fusion.30
  116.8 2.6 select_reduce_fusion
  119.5 3.2 multiply_reduce_fusion
  122.7 1.3 copy-done.6
  124.1 1.6 multiply_reduce_fusion.2
  125.7 0.7 divide_convert_fusion
  126.4 1.0 copy.22
  127.4 1.4 convolution_multiply_fusion
  128.9 0.1 pad.6
  128.9 4.4 %fusion.6 = bf16[1024,1024]{1,0:T(8,128)(2,1)S(1)} fusion(f32[1024,1024]{1,0:T(8,128)} %get-tuple-element.34, f32[64,1024]{1,0:T(8,128)S(1)} %convolution_multiply_fusion), kind=kLoop, calls=%fused_computation.13 | loop fusion | flops 20971520 | bytes 6553600 | tf_op jit(solution)/shard_map/convert_element_type | solution.py:60
  133.4 10.5 %convolution_convert_fusion = bf16[3072,1024]{1,0:T(8,128)(2,1)} fusion(bf16[1024,1024]{1,0:T(8,128)(2,1)S(1)} %fusion.6, bf16[1024,1024]{1,0:T(8,128)(2,1)S(1)} %bitcast.61, bf16[1024,1024]{1,0:T(8,128)(2,1)S(1)} %bitcast.56, bf16[1024,1024]{1,0:T(8,128)(2,1)S(1)} %bitcast.59), kind=kOutput, calls=%fused_computation.6 | convolution fusion | flops 6464471040 | bytes 14680064 | tf_op jit(solution)/shard_map/dot_general | solution.py:61
  143.9 0.8 convolution_convert_fusion.1
  144.6 3.2 copy.24
  147.8 11.0 %copy.23 = bf16[16,192,1024]{1,2,0:T(8,128)(2,1)} copy(bf16[16,192,1024]{2,1,0:T(8,128)(2,1)} %bitcast.57) | data formatting | bytes 12582912 | tf_op jit(solution)/shard_map/reshape | solution.py:143
  158.8 0.2 select_reduce_fusion.2
  159.0 10.4 %pad_maximum_fusion = bf16[16,256,1024]{1,2,0:T(8,128)(2,1)} fusion(bf16[16,64,1024]{1,2,0:T(8,128)(2,1)} %copy.24, bf16[16,192,1024]{1,2,0:T(8,128)(2,1)} %copy.23), kind=kLoop, calls=%fused_computation | loop fusion | flops 16777216 | bytes 16777216 | tf_op jit(solution)/shard_map/concatenate | solution.py:141
  169.5 0.0 reduce-scatter.5.cloned.1.call-start
  169.5 33.8 %psum.15 = f32[2,100]{1,0:T(2,128)S(1)} all-reduce(f32[2,100]{1,0:T(2,128)S(1)} %pad_maximum_fusion.5), channel_id=1, replica_groups=mesh['blk'=16,'dp'=16] {'dp'}, use_global_device_ids=true, to_apply=%region_17.18 | all-reduce | flops 200 | bytes 1600 | tf_op jit(solution)/shard_map/psum | solution.py:151
  203.3 0.5 broadcast_subtract_fusion
  203.9 145.1 %reduce-scatter.3.cloned.1.call-done = bf16[1,256,1024]{1,2,0:T(8,128)(2,1)} async-done(((bf16[16,256,1024]{1,2,0:T(8,128)(2,1)}), bf16[1,256,1024]{1,2,0:T(8,128)(2,1)}) %reduce-scatter.3.cloned.1.call-update) | async-done | bytes 524304 | tf_op jit(solution)/shard_map/reduce_scatter | solution.py:149
  349.0 0.6 add_reduce_fusion
  349.6 0.5 slice_bitcast_fusion
  350.1 1.9 multiply_reduce_fusion.1
  352.0 0.8 divide_bitcast_fusion
  352.8 74.3 %reduce-scatter.5.cloned.1.call-done = bf16[256,64]{0,1:T(8,128)(2,1)} async-done(((bf16[256,1024]{0,1:T(8,128)(2,1)}), bf16[256,64]{0,1:T(8,128)(2,1)}) %reduce-scatter.5.cloned.1.call-update) | async-done | bytes 32784 | tf_op jit(solution)/shard_map/reduce_scatter | solution.py:150
  427.0 1.4 slice_convert_fusion.1
  428.4 1.4 slice_convert_fusion
  (36 shorter events, 0.1 us)
Async XLA Ops:
  7.2 20.8 %copy-start = (bf16[1024,512]{1,0:T(8,128)(2,1)S(1)}, bf16[1024,512]{1,0:T(8,128)(2,1)}, u32[]{:S(2)}) copy-start(bf16[1024,512]{1,0:T(8,128)(2,1)} %param.10) | copy-start | bytes 3145732
  7.2 104.6 %all-gather.2.cloned.1.call-start = ((), (), s32[]{:S(2)}) async-start(), calls=%async_computation.2 | async-start | bytes 2506752 | tf_op jit(solution)/shard_map/all_gather | solution.py:87
  13.5 1.6 copy-start.1
  13.5 4.9 %copy-start.15 = (bf16[3072,1024]{1,0:T(8,128)(2,1)S(1)}, bf16[3072,1024]{1,0:T(8,128)(2,1)}, u32[]{:S(2)}) copy-start(bf16[3072,1024]{1,0:T(8,128)(2,1)} %param.9) | copy-start | bytes 18874372
  14.4 13.6 %copy-start.2 = (bf16[64,16,1024]{2,1,0:T(8,128)(2,1)}, bf16[64,16,1024]{2,1,0:T(8,128)(2,1)S(1)}, u32[]{:S(2)}) copy-start(bf16[64,16,1024]{2,1,0:T(8,128)(2,1)S(1)} %concatenate.22) | copy-start | bytes 6291460
  14.8 13.2 %copy-start.4 = (bf16[64,16,1024]{2,1,0:T(8,128)(2,1)}, bf16[64,16,1024]{2,1,0:T(8,128)(2,1)S(1)}, u32[]{:S(2)}) copy-start(bf16[64,16,1024]{2,1,0:T(8,128)(2,1)S(1)} %concatenate.25) | copy-start | bytes 6291460
  18.4 10.0 %copy-start.7 = (bf16[1,64,512]{2,1,0:T(8,128)(2,1)S(1)}, bf16[1,64,512]{2,1,0:T(8,128)(2,1)}, u32[]{:S(2)}) copy-start(bf16[1,64,512]{2,1,0:T(8,128)(2,1)} %param.11) | copy-start | bytes 196612
  18.4 94.5 %copy-start.11 = (f32[100]{0:T(128)S(1)}, f32[100]{0:T(128)}, u32[]{:S(2)}) copy-start(f32[100]{0:T(128)} %param.14) | copy-start | bytes 1204
  28.4 83.4 %copy-start.9 = (f32[64]{0:T(128)}, f32[64]{0:T(128)S(1)}, u32[]{:S(2)}) copy-start(f32[64]{0:T(128)S(1)} %add_sqrt_fusion.1) | copy-start | bytes 772
  29.3 319.7 %reduce-scatter.3.cloned.1.call-start = ((), (), s32[]{:S(2)}) async-start(), calls=%async_computation.3 | async-start | bytes 8912896 | tf_op jit(solution)/shard_map/reduce_scatter | solution.py:149
  110.6 6.2 %copy-start.13 = (f32[100]{0:T(128)}, f32[100]{0:T(128)S(1)}, u32[]{:S(2)}) copy-start(f32[100]{0:T(128)S(1)} %psum.14) | copy-start | bytes 1204
  119.5 4.6 %copy-start.10 = (f32[64]{0:T(128)S(1)}, f32[64]{0:T(128)}, u32[]{:S(2)}) copy-start(f32[64]{0:T(128)} %copy-done.9) | copy-start | bytes 772
  122.7 1.3 copy-start.6
  127.4 5.9 %copy-start.3 = (bf16[64,16,1024]{2,1,0:T(8,128)(2,1)S(1)}, bf16[64,16,1024]{2,1,0:T(8,128)(2,1)}, u32[]{:S(2)}) copy-start(bf16[64,16,1024]{2,1,0:T(8,128)(2,1)} %copy-done.2) | copy-start | bytes 6291460
  127.4 5.9 %copy-start.5 = (bf16[64,16,1024]{2,1,0:T(8,128)(2,1)S(1)}, bf16[64,16,1024]{2,1,0:T(8,128)(2,1)}, u32[]{:S(2)}) copy-start(bf16[64,16,1024]{2,1,0:T(8,128)(2,1)} %copy-done.4) | copy-start | bytes 6291460
  169.4 33.9 %copy-start.12 = (f32[100]{0:T(128)S(1)}, f32[100]{0:T(128)}, u32[]{:S(2)}) copy-start(f32[100]{0:T(128)} %param.15) | copy-start | bytes 1204
  169.4 33.9 %copy-start.14 = (f32[100]{0:T(128)S(1)}, f32[100]{0:T(128)}, u32[]{:S(2)}) copy-start(f32[100]{0:T(128)} %copy-done.13) | copy-start | bytes 1204
  169.4 180.7 %copy-start.8 = (bf16[1,64,512]{2,1,0:T(8,128)(2,1)S(1)}, bf16[1,64,512]{2,1,0:T(8,128)(2,1)}, u32[]{:S(2)}) copy-start(bf16[1,64,512]{2,1,0:T(8,128)(2,1)} %param.11) | copy-start | bytes 196612
  169.5 257.6 %reduce-scatter.5.cloned.1.call-start = ((), (), s32[]{:S(2)}) async-start(), calls=%async_computation.4 | async-start | bytes 557056 | tf_op jit(solution)/shard_map/reduce_scatter | solution.py:150
Sparse Core Ops, SparseCore 0:
  29.4 77.0 all-gather.1
  169.6 179.3 reduce-scatter.2
  353.0 73.9 reduce-scatter.4

commit v4 on v2

--- a/solution.py
+++ b/solution.py
@@ -77,6 +77,26 @@
         proj_part.reshape(n_dp, n_blk, pad_rows, seg).transpose(0, 2, 1, 3).reshape(n_dp, pad_rows, width)
     )
     return jnp.concatenate([conv_part, proj_part], axis=1), per_block
+
+
+def halving_scatter(rows, split, n_blk):
+    me = lax.axis_index("blk")
+    parts = [rows[:split], rows[split:]]
+    parts = [p.reshape(p.shape[0], n_blk, -1).astype(jnp.float32) for p in parts]
+    bit = 1
+    while bit < n_blk:
+        mine = (me // bit) % 2
+        pairs = [(i, i ^ bit) for i in range(n_blk)]
+        kept = []
+        for p in parts:
+            grouped = p.reshape(p.shape[0], p.shape[1] // 2, 2, p.shape[2])
+            keep = lax.dynamic_index_in_dim(grouped, mine, axis=2, keepdims=False)
+            send = lax.dynamic_index_in_dim(grouped, 1 - mine, axis=2, keepdims=False)
+            got = lax.ppermute(send.astype(jnp.bfloat16), "blk", pairs)
+            kept.append(keep + got.astype(jnp.float32))
+        parts = kept
+        bit *= 2
+    return [p[:, 0, :] for p in parts]
 
 
 def local(
@@ -154,15 +174,14 @@
     buf, per_block = scatter_buffer(conv_term_t, proj_term_t, n_blk, n_dp)
     buf, batch_sums = lax.optimization_barrier((buf, batch_sums))
     stage = lax.psum_scatter(buf, "dp", scatter_dimension=0, tiled=True)
-    stage = lax.psum_scatter(stage[0], "blk", scatter_dimension=1, tiled=True)
     loss_sum, scale_grad = lax.psum(batch_sums, "dp")
     conv_cols = conv_term_t.shape[0] // n_dp
-    conv_grad = stage[:conv_cols].T.astype(jnp.float32)
+    conv_part, proj_part = halving_scatter(stage[0], conv_cols, n_blk)
+    conv_grad = conv_part.T
     proj_grad = (
-        stage[conv_cols:]
-        .reshape(-1)[:per_block]
+        proj_part.reshape(-1)[:per_block]
         .reshape(proj_term_t.shape[0] // n_dp, proj_term_t.shape[1] // n_blk)
-        .T.astype(jnp.float32)
+        .T
     )
     var_weight = jnp.exp(-log_var)
     lang_mean = loss_sum / jnp.maximum(counts, 1.0)

time: 349 us -> 311 us (0.89)
  waiting for transfers between devices: 137 us -> 84.2 us
  starting transfers between devices: 0.12 us -> 16.1 us
    unnamed x4 -> x2, waiting for transfers between devices: 67.1 us -> 0.03 us
    ppermute x0 -> x8, waiting for transfers between devices: none -> 18.2 us  [halving_scatter(): got = lax.ppermute(send.astype(jnp.bfloat16), 'blk', pairs)]
    ppermute x0 -> x8, starting transfers between devices: none -> 16 us  [halving_scatter(): got = lax.ppermute(send.astype(jnp.bfloat16), 'blk', pairs)]
    reduce_scatter x1, waiting for transfers between devices: 70.4 us -> 65.9 us  [local(): stage = lax.psum_scatter(buf, 'dp', scatter_dimension=0, tiled=True)]
  transfers between devices with their start and end apart: 3 -> 10, of which waited for: 2 -> 7; matrix products, arithmetic and copies ran while one was open for 2% -> 4% of each run, Pallas kernels for 0% -> 0%
where the time goes in v4:
time: 311 us; the launch traced here: 310 us
  blocking collectives  111 us (36%)
  waiting for transfers between devices  84.2 us (27%)
  local copies, waits for them, and re-layouts  32 us (10%)
  matrix products  27.3 us (9%)
  other arithmetic  25 us (8%)
  starting transfers between devices  16.1 us (5%)
  between operations  14.7 us (5%)
    psum x1, blocking collectives, local(): counts = lax.psum(local_counts, ('blk', 'dp'))  80.2 us
    reduce_scatter x1, waiting for transfers between devices, local(): stage = lax.psum_scatter(buf, 'dp', scatter_dimension=0, tiled=True)  65.9 us
    psum x1, blocking collectives, local(): loss_sum, scale_grad = lax.psum(batch_sums, 'dp')  30.4 us
    ppermute x8, waiting for transfers between devices, halving_scatter(): got = lax.ppermute(send.astype(jnp.bfloat16), 'blk', pairs)  18.2 us
    ppermute x8, starting transfers between devices, halving_scatter(): got = lax.ppermute(send.astype(jnp.bfloat16), 'blk', pairs)  16 us
    dot_general x1, matrix products, encode_back(): lax.dot_general(grad_pre, stacked, (((0,), (0,)), ((), ())), preferred_el...  9.38 us
    dot_general x1, matrix products, encode(): preact = jnp.dot(stacked, conv_weight, preferred_element_type=jnp.float32)  9.34 us
    reshape x2, local copies, waits for them, and re-layouts, scatter_buffer(): proj_part.reshape(n_dp, n_blk, pad_rows, seg).transpose(0, 2, 1, 3)  7.38 us
  transfers between devices with their start and end apart: 10, of which 7 were waited for; matrix products, arithmetic and copies ran while one was open for 4% of the time, Pallas kernels for 0%

profile of v4, /device:TPU:8, one launch (start us, length us, event | category | flops | bytes accessed | tf_op | source)
XLA Modules:
  0.0 309.9 jit_solution(14148215095979899908)
XLA Ops:
  7.2 3.3 %fusion.36 = (bf16[64,15,1024]{2,1,0:T(8,128)(2,1)S(1)}, bf16[64,15,1024]{2,1,0:T(8,128)(2,1)S(1)}) fusion(bf16[64,16,1024]{2,1,0:T(8,128)(2,1)} %bitcast.94), kind=kLoop, calls=%fused_computation.114 | loop fusion | bytes 7864320 | tf_op jit(solution)/shard_map/slice | solution.py:12
  10.6 0.9 concatenate.22
  12.2 3.3 %copy-done.17 = bf16[3072,1024]{1,0:T(8,128)(2,1)S(1)} copy-done((bf16[3072,1024]{1,0:T(8,128)(2,1)S(1)}, bf16[3072,1024]{1,0:T(8,128)(2,1)}, u32[]{:S(2)}) %copy-start.17) | copy-done | bytes 6291480
  15.5 9.3 %bitcast_reduce_fusion = (f32[64,1024]{1,0:T(8,128)S(1)}, f32[1024,1024]{1,0:T(8,128)}) fusion(bf16[3072,1024]{1,0:T(8,128)(2,1)S(1)} %copy-done.17, bf16[1024,1024]{1,0:T(8,128)(2,1)S(1)} %bitcast.101, bf16[1024,1024]{1,0:T(8,128)(2,1)S(1)} %bitcast.95, bf16[1024,1024]{1,0:T(8,128)(2,1)S(1)} %bitcast.99), kind=kOutput, calls=%fused_computation.17 | convolution fusion | flops 6470696960 | bytes 17039360 | tf_op jit(solution)/shard_map/dot_general | solution.py:22
  25.5 0.6 convert_reduce_fusion.1
  26.2 0.7 pad_maximum_fusion.4
  27.0 1.2 exp.20
  28.2 80.2 %psum.14 = f32[100]{0:T(128)S(1)} all-reduce(f32[100]{0:T(128)} %convert_reduce_fusion.1), channel_id=1, replica_groups=mesh['blk'=16,'dp'=16] {'blk','dp'}, use_global_device_ids=true, to_apply=%region_4.0 | all-reduce | flops 100 | bytes 800 | tf_op jit(solution)/shard_map/psum | solution.py:123
  108.4 1.2 maximum_divide_fusion
  109.6 1.2 convert_reduce_fusion
  110.7 0.9 select_reduce_fusion.5
  111.6 3.0 fusion.34
  114.6 2.6 select_reduce_fusion
  117.3 3.2 %multiply_reduce_fusion = (f32[1024]{0:T(1024)S(1)}, bf16[1024,1024]{1,0:T(8,128)(2,1)S(1)}) fusion(f32[1024,1024]{1,0:T(8,128)S(1)} %get-tuple-element.37, f32[1024]{0:T(1024)S(1)} %get-tuple-element.28, f32[1024]{0:T(1024)S(1)} %get-tuple-element.21, f32[1024]{0:T(1024)S(1)} %get-tuple-element.27, f32[1024]{0:T(1024)S(1)} %get-tuple-element.22, ...), kind=kLoop, calls=%fused_computation.18 | loop fusion | flops 14679040 | bytes 6316032 | tf_op jit(solution)/shard_map/reduce_sum | solution.py:153
  120.5 2.4 multiply_reduce_fusion.2
  124.0 2.8 fusion.6
  126.8 9.4 %convolution_convert_fusion = bf16[1024,3072]{1,0:T(8,128)(2,1)} fusion(bf16[1024,1024]{1,0:T(8,128)(2,1)S(1)} %fusion.6, bf16[1024,1024]{1,0:T(8,128)(2,1)S(1)} %bitcast.102, bf16[1024,1024]{1,0:T(8,128)(2,1)S(1)} %bitcast.96, bf16[1024,1024]{1,0:T(8,128)(2,1)S(1)} %bitcast.100), kind=kOutput, calls=%fused_computation.6 | convolution fusion | flops 6464471040 | bytes 14680064 | tf_op jit(solution)/shard_map/dot_general | solution.py:55
  136.2 1.3 reshape.150
  137.6 1.9 copy.55
  139.4 3.4 %reshape.151 = bf16[16,16,2048]{2,1,0:T(8,128)(2,1)S(1)} reshape(bf16[16,16,32,64]{3,2,1,0:T(8,128)(2,1)} %bitcast.97) | data formatting | bytes 2097152 | tf_op jit(solution)/shard_map/reshape | solution.py:73
  142.8 1.3 pad.6
  144.2 3.7 %reshape.152 = bf16[16,16,16,192]{3,2,1,0:T(8,128)(2,1)S(1)} reshape(bf16[16,16,3072]{2,1,0:T(8,128)(2,1)} %pad.6) | data formatting | bytes 3145728 | tf_op jit(solution)/shard_map/reshape | solution.py:77
  147.9 2.2 copy.30
  150.1 3.7 %reshape.153 = bf16[16,16,3072]{2,1,0:T(8,128)(2,1)S(1)} reshape(bf16[16,16,16,192]{3,2,1,0:T(8,128)(2,1)} %copy.30) | data formatting | bytes 3145728 | tf_op jit(solution)/shard_map/reshape | solution.py:77
  154.0 6.8 %pad_maximum_fusion = bf16[16,80,3072]{2,1,0:T(8,128)(2,1)} fusion(bf16[16,16,3072]{2,1,0:T(8,128)(2,1)S(1)} %reshape.153, bf16[16,64,3072]{2,1,0:T(8,128)(2,1)} %bitcast.98), kind=kLoop, calls=%fused_computation | loop fusion | flops 15728640 | bytes 15728640 | tf_op jit(solution)/shard_map/concatenate | solution.py:79
  160.9 30.4 %psum.15 = f32[2,100]{1,0:T(2,128)S(1)} all-reduce(f32[2,100]{1,0:T(2,128)S(1)} %pad_maximum_fusion.5), channel_id=1, replica_groups=mesh['blk'=16,'dp'=16] {'dp'}, use_global_device_ids=true, to_apply=%region_17.18 | all-reduce | flops 200 | bytes 1600 | tf_op jit(solution)/shard_map/psum | solution.py:177
  191.8 0.6 add_reduce_fusion
  192.9 1.9 multiply_reduce_fusion.1
  194.8 0.8 divide_bitcast_fusion
  195.5 65.9 %reduce-scatter.2.cloned.1.call-done = bf16[1,80,3072]{2,1,0:T(8,128)(2,1)} async-done(((bf16[16,80,3072]{2,1,0:T(8,128)(2,1)}), bf16[1,80,3072]{2,1,0:T(8,128)(2,1)}) %reduce-scatter.2.cloned.1.call-update) | async-done | bytes 491536 | tf_op jit(solution)/shard_map/reduce_scatter | solution.py:176
  261.5 0.9 slice_convert_fusion.1
  262.8 0.6 collective-permute-start.4
  263.4 1.0 slice_convert_fusion
  264.5 1.0 reshape.160
  266.2 1.0 collective-permute-done.4
  267.3 1.6 collective-permute-start.5
  269.0 2.5 collective-permute-done.5
  271.5 2.4 collective-permute-start.6
  274.6 0.8 collective-permute-start
  275.4 0.8 collective-permute-done.6
  276.3 6.2 %collective-permute-start.7 = (bf16[16,1,192]{2,0,1:T(8,128)(2,1)S(1)}, bf16[16,1,192]{2,0,1:T(8,128)(2,1)S(1)}, u32[]{:S(2)}, u32[]{:S(2)}) collective-permute-start(bf16[16,1,192]{2,0,1:T(8,128)(2,1)S(1)} %dynamic-slice_convert_fusion.5), channel_id=1, source_target_pairs={{0,128},{16,144},{32,160},{48,176},{64,192},{80,208},{96,224},{112... | collective-permute-start | bytes 18440 | tf_op jit(solution)/shard_map/ppermute | solution.py:95
  283.9 4.3 %collective-permute-done.1 = bf16[64,4,192]{2,0,1:T(8,128)(2,1)S(1)} collective-permute-done((bf16[64,4,192]{2,0,1:T(8,128)(2,1)S(1)}, bf16[64,4,192]{2,0,1:T(8,128)(2,1)S(1)}, u32[]{:S(2)}, u32[]{:S(2)}) %collective-permute-start.1) | collective-permute-done | bytes 98336 | tf_op jit(solution)/shard_map/ppermute | solution.py:95
  288.3 0.7 collective-permute-start.2
  289.1 5.4 %collective-permute-done.2 = bf16[64,2,192]{2,0,1:T(8,128)(2,1)S(1)} collective-permute-done((bf16[64,2,192]{2,0,1:T(8,128)(2,1)S(1)}, bf16[64,2,192]{2,0,1:T(8,128)(2,1)S(1)}, u32[]{:S(2)}, u32[]{:S(2)}) %collective-permute-start.2) | collective-permute-done | bytes 49184 | tf_op jit(solution)/shard_map/ppermute | solution.py:95
  294.5 3.1 %collective-permute-start.3 = (bf16[64,1,192]{2,0,1:T(8,128)(2,1)S(1)}, bf16[64,1,192]{2,0,1:T(8,128)(2,1)S(1)}, u32[]{:S(2)}, u32[]{:S(2)}) collective-permute-start(bf16[64,1,192]{2,0,1:T(8,128)(2,1)S(1)} %dynamic-slice_convert_fusion.3), channel_id=1, source_target_pairs={{0,128},{16,144},{32,160},{48,176},{64,192},{80,208},{96,224},{112... | collective-permute-start | bytes 73736 | tf_op jit(solution)/shard_map/ppermute | solution.py:95
  297.6 0.6 slice_bitcast_fusion
  298.2 4.2 %collective-permute-done.3 = bf16[64,1,192]{2,0,1:T(8,128)(2,1)S(1)} collective-permute-done((bf16[64,1,192]{2,0,1:T(8,128)(2,1)S(1)}, bf16[64,1,192]{2,0,1:T(8,128)(2,1)S(1)}, u32[]{:S(2)}, u32[]{:S(2)}) %collective-permute-start.3) | collective-permute-done | bytes 24608 | tf_op jit(solution)/shard_map/ppermute | solution.py:95
  302.4 0.6 add_bitcast_fusion
  (87 shorter events, 7.2 us)
Async XLA Ops:
  7.2 17.7 %copy-start = (bf16[1024,512]{1,0:T(8,128)(2,1)S(1)}, bf16[1024,512]{1,0:T(8,128)(2,1)}, u32[]{:S(2)}) copy-start(bf16[1024,512]{1,0:T(8,128)(2,1)} %param.10) | copy-start | bytes 3145732
  7.2 102.4 %all-gather.2.cloned.1.call-start = ((), (), s32[]{:S(2)}) async-start(), calls=%async_computation.1 | async-start | bytes 2506752 | tf_op jit(solution)/shard_map/all_gather | solution.py:122
  10.6 1.6 copy-start.2
  10.6 4.9 %copy-start.17 = (bf16[3072,1024]{1,0:T(8,128)(2,1)S(1)}, bf16[3072,1024]{1,0:T(8,128)(2,1)}, u32[]{:S(2)}) copy-start(bf16[3072,1024]{1,0:T(8,128)(2,1)} %param.9) | copy-start | bytes 18874372
  11.5 13.4 %copy-start.5 = (bf16[64,16,1024]{2,1,0:T(8,128)(2,1)}, bf16[64,16,1024]{2,1,0:T(8,128)(2,1)S(1)}, u32[]{:S(2)}) copy-start(bf16[64,16,1024]{2,1,0:T(8,128)(2,1)S(1)} %concatenate.22) | copy-start | bytes 6291460
  11.9 13.0 %copy-start.7 = (bf16[64,16,1024]{2,1,0:T(8,128)(2,1)}, bf16[64,16,1024]{2,1,0:T(8,128)(2,1)S(1)}, u32[]{:S(2)}) copy-start(bf16[64,16,1024]{2,1,0:T(8,128)(2,1)S(1)} %concatenate.25) | copy-start | bytes 6291460
  15.5 9.8 %copy-start.9 = (bf16[1,64,512]{2,1,0:T(8,128)(2,1)S(1)}, bf16[1,64,512]{2,1,0:T(8,128)(2,1)}, u32[]{:S(2)}) copy-start(bf16[1,64,512]{2,1,0:T(8,128)(2,1)} %param.11) | copy-start | bytes 196612
  15.5 9.9 %copy-start.18 = (s32[1,64]{1,0:T(1,128)S(1)}, s32[1,64]{1,0:T(1,128)}, u32[]{:S(2)}) copy-start(s32[1,64]{1,0:T(1,128)} %param.12) | copy-start | bytes 772
  15.5 95.2 %copy-start.13 = (f32[100]{0:T(128)S(1)}, f32[100]{0:T(128)}, u32[]{:S(2)}) copy-start(f32[100]{0:T(128)} %param.14) | copy-start | bytes 1204
  25.3 84.3 %copy-start.11 = (f32[64]{0:T(128)}, f32[64]{0:T(128)S(1)}, u32[]{:S(2)}) copy-start(f32[64]{0:T(128)S(1)} %add_sqrt_fusion.1) | copy-start | bytes 772
  26.9 234.5 %reduce-scatter.2.cloned.1.call-start = ((), (), s32[]{:S(2)}) async-start(), calls=%async_computation.2 | async-start | bytes 8355840 | tf_op jit(solution)/shard_map/reduce_scatter | solution.py:176
  108.4 6.2 %copy-start.15 = (f32[100]{0:T(128)}, f32[100]{0:T(128)S(1)}, u32[]{:S(2)}) copy-start(f32[100]{0:T(128)S(1)} %psum.14) | copy-start | bytes 1204
  117.3 3.3 %copy-start.12 = (f32[64]{0:T(128)S(1)}, f32[64]{0:T(128)}, u32[]{:S(2)}) copy-start(f32[64]{0:T(128)} %copy-done.11) | copy-start | bytes 772
  117.3 6.7 %copy-start.3 = (f32[1024,1024]{1,0:T(8,128)S(1)}, f32[1024,1024]{1,0:T(8,128)}, u32[]{:S(2)}) copy-start(f32[1024,1024]{1,0:T(8,128)} %get-tuple-element.34) | copy-start | bytes 12582916
  120.5 3.4 %copy-start.4 = (bf16[1024,1024]{1,0:T(8,128)(2,1)}, bf16[1024,1024]{1,0:T(8,128)(2,1)S(1)}, u32[]{:S(2)}) copy-start(bf16[1024,1024]{1,0:T(8,128)(2,1)S(1)} %get-tuple-element.30) | copy-start | bytes 6291460
  123.4 3.4 %copy-start.6 = (bf16[64,16,1024]{2,1,0:T(8,128)(2,1)S(1)}, bf16[64,16,1024]{2,1,0:T(8,128)(2,1)}, u32[]{:S(2)}) copy-start(bf16[64,16,1024]{2,1,0:T(8,128)(2,1)} %copy-done.5) | copy-start | bytes 6291460
  123.4 3.4 %copy-start.8 = (bf16[64,16,1024]{2,1,0:T(8,128)(2,1)S(1)}, bf16[64,16,1024]{2,1,0:T(8,128)(2,1)}, u32[]{:S(2)}) copy-start(bf16[64,16,1024]{2,1,0:T(8,128)(2,1)} %copy-done.7) | copy-start | bytes 6291460
  160.8 30.5 %copy-start.14 = (f32[100]{0:T(128)S(1)}, f32[100]{0:T(128)}, u32[]{:S(2)}) copy-start(f32[100]{0:T(128)} %param.15) | copy-start | bytes 1204
  160.8 30.5 %copy-start.16 = (f32[100]{0:T(128)S(1)}, f32[100]{0:T(128)}, u32[]{:S(2)}) copy-start(f32[100]{0:T(128)} %copy-done.15) | copy-start | bytes 1204
  160.8 32.2 %copy-start.10 = (bf16[1,64,512]{2,1,0:T(8,128)(2,1)S(1)}, bf16[1,64,512]{2,1,0:T(8,128)(2,1)}, u32[]{:S(2)}) copy-start(bf16[1,64,512]{2,1,0:T(8,128)(2,1)} %param.11) | copy-start | bytes 196612
  262.8 4.4 %collective-permute-start.4 = (bf16[16,8,192]{2,1,0:T(8,128)(2,1)S(1)}, bf16[16,8,192]{2,1,0:T(8,128)(2,1)S(1)}, u32[]{:S(2)}, u32[]{:S(2)}) collective-permute-start(bf16[16,8,192]{2,1,0:T(8,128)(2,1)S(1)} %bitcast.109), channel_id=1, source_target_pairs={{0,16},{16,0},{32,48},{48,32},{64,80},{80,64},{96,112},{112,96},{1... | collective-permute-start | bytes 147464 | tf_op jit(solution)/shard_map/ppermute | solution.py:95
  266.0 37.1 %copy-start.1 = (bf16[1024,512]{1,0:T(8,128)(2,1)S(1)}, bf16[1024,512]{1,0:T(8,128)(2,1)}, u32[]{:S(2)}) copy-start(bf16[1024,512]{1,0:T(8,128)(2,1)} %param.10) | copy-start | bytes 3145732
  267.3 4.2 %collective-permute-start.5 = (bf16[16,4,192]{2,0,1:T(8,128)(2,1)S(1)}, bf16[16,4,192]{2,0,1:T(8,128)(2,1)S(1)}, u32[]{:S(2)}, u32[]{:S(2)}) collective-permute-start(bf16[16,4,192]{2,0,1:T(8,128)(2,1)S(1)} %bitcast.110), channel_id=1, source_target_pairs={{0,32},{16,48},{32,0},{48,16},{64,96},{80,112},{96,64},{112,80},{1... | collective-permute-start | bytes 73736 | tf_op jit(solution)/shard_map/ppermute | solution.py:95
  271.5 4.7 %collective-permute-start.6 = (bf16[16,2,192]{2,0,1:T(8,128)(2,1)S(1)}, bf16[16,2,192]{2,0,1:T(8,128)(2,1)S(1)}, u32[]{:S(2)}, u32[]{:S(2)}) collective-permute-start(bf16[16,2,192]{2,0,1:T(8,128)(2,1)S(1)} %fusion.24), channel_id=1, source_target_pairs={{0,64},{16,80},{32,96},{48,112},{64,0},{80,16},{96,32},{112,48},{1... | collective-permute-start | bytes 36872 | tf_op jit(solution)/shard_map/ppermute | solution.py:95
  274.6 8.0 %collective-permute-start = (bf16[64,8,192]{2,1,0:T(8,128)(2,1)S(1)}, bf16[64,8,192]{2,1,0:T(8,128)(2,1)S(1)}, u32[]{:S(2)}, u32[]{:S(2)}) collective-permute-start(bf16[64,8,192]{2,1,0:T(8,128)(2,1)S(1)} %bitcast.105), channel_id=1, source_target_pairs={{0,16},{16,0},{32,48},{48,32},{64,80},{80,64},{96,112},{112,96},{1... | collective-permute-start | bytes 589832 | tf_op jit(solution)/shard_map/ppermute | solution.py:95
  276.3 12.7 %collective-permute-start.7 = (bf16[16,1,192]{2,0,1:T(8,128)(2,1)S(1)}, bf16[16,1,192]{2,0,1:T(8,128)(2,1)S(1)}, u32[]{:S(2)}, u32[]{:S(2)}) collective-permute-start(bf16[16,1,192]{2,0,1:T(8,128)(2,1)S(1)} %dynamic-slice_convert_fusion.5), channel_id=1, source_target_pairs={{0,128},{16,144},{32,160},{48,176},{64,192},{80,208},{96,224},{112... | collective-permute-start | bytes 18440 | tf_op jit(solution)/shard_map/ppermute | solution.py:95
  283.2 5.1 %collective-permute-start.1 = (bf16[64,4,192]{2,0,1:T(8,128)(2,1)S(1)}, bf16[64,4,192]{2,0,1:T(8,128)(2,1)S(1)}, u32[]{:S(2)}, u32[]{:S(2)}) collective-permute-start(bf16[64,4,192]{2,0,1:T(8,128)(2,1)S(1)} %bitcast.108), channel_id=1, source_target_pairs={{0,32},{16,48},{32,0},{48,16},{64,96},{80,112},{96,64},{112,80},{1... | collective-permute-start | bytes 294920 | tf_op jit(solution)/shard_map/ppermute | solution.py:95
  288.3 6.1 %collective-permute-start.2 = (bf16[64,2,192]{2,0,1:T(8,128)(2,1)S(1)}, bf16[64,2,192]{2,0,1:T(8,128)(2,1)S(1)}, u32[]{:S(2)}, u32[]{:S(2)}) collective-permute-start(bf16[64,2,192]{2,0,1:T(8,128)(2,1)S(1)} %fusion.21), channel_id=1, source_target_pairs={{0,64},{16,80},{32,96},{48,112},{64,0},{80,16},{96,32},{112,48},{1... | collective-permute-start | bytes 147464 | tf_op jit(solution)/shard_map/ppermute | solution.py:95
  294.5 7.9 %collective-permute-start.3 = (bf16[64,1,192]{2,0,1:T(8,128)(2,1)S(1)}, bf16[64,1,192]{2,0,1:T(8,128)(2,1)S(1)}, u32[]{:S(2)}, u32[]{:S(2)}) collective-permute-start(bf16[64,1,192]{2,0,1:T(8,128)(2,1)S(1)} %dynamic-slice_convert_fusion.3), channel_id=1, source_target_pairs={{0,128},{16,144},{32,160},{48,176},{64,192},{80,208},{96,224},{112... | collective-permute-start | bytes 73736 | tf_op jit(solution)/shard_map/ppermute | solution.py:95
Sparse Core Ops, SparseCore 0:
  27.1 77.5 all-gather.1
  160.9 100.5 reduce-scatter.1

commit v5 on v4

--- a/solution.py
+++ b/solution.py
@@ -58,30 +58,18 @@
     return (conv_term_t, proj_term_t)
 
 
-def scatter_buffer(conv_term_t, proj_term_t, n_blk, n_dp):
-    width = conv_term_t.shape[1]
-    conv_part = conv_term_t.astype(jnp.bfloat16).reshape(n_dp, -1, width)
-    p_cols, p_rows = proj_term_t.shape
-    per_block = (p_cols // n_dp) * (p_rows // n_blk)
-    seg = width // n_blk
-    pad_rows = -(-per_block // seg)
-    pad_rows = -(-pad_rows // 16) * 16
-    proj_part = (
-        proj_term_t.astype(jnp.bfloat16)
-        .reshape(n_dp, p_cols // n_dp, n_blk, p_rows // n_blk)
-        .transpose(0, 2, 1, 3)
-        .reshape(n_dp, n_blk, per_block)
-    )
-    proj_part = jnp.pad(proj_part, ((0, 0), (0, 0), (0, pad_rows * seg - per_block)))
-    proj_part = (
-        proj_part.reshape(n_dp, n_blk, pad_rows, seg).transpose(0, 2, 1, 3).reshape(n_dp, pad_rows, width)
-    )
-    return jnp.concatenate([conv_part, proj_part], axis=1), per_block
-
-
-def halving_scatter(rows, split, n_blk):
+def scatter_buffer(conv_term_t, proj_term_t, n_dp):
+    return jnp.concatenate(
+        [
+            conv_term_t.astype(jnp.bfloat16).reshape(n_dp, -1),
+            proj_term_t.astype(jnp.bfloat16).reshape(n_dp, -1),
+        ],
+        axis=1,
+    )
+
+
+def halving_scatter(parts, n_blk):
     me = lax.axis_index("blk")
-    parts = [rows[:split], rows[split:]]
     parts = [p.reshape(p.shape[0], n_blk, -1).astype(jnp.float32) for p in parts]
     bit = 1
     while bit < n_blk:
@@ -171,18 +159,22 @@
     conv_term_t, proj_term_t = encode_back(
         stacked, preact, pooled, audio_unit, audio_len, grad_audio, proj_weight
     )
-    buf, per_block = scatter_buffer(conv_term_t, proj_term_t, n_blk, n_dp)
+    buf = scatter_buffer(conv_term_t, proj_term_t, n_dp)
     buf, batch_sums = lax.optimization_barrier((buf, batch_sums))
     stage = lax.psum_scatter(buf, "dp", scatter_dimension=0, tiled=True)
     loss_sum, scale_grad = lax.psum(batch_sums, "dp")
     conv_cols = conv_term_t.shape[0] // n_dp
-    conv_part, proj_part = halving_scatter(stage[0], conv_cols, n_blk)
+    proj_cols = proj_term_t.shape[0] // n_dp
+    conv_size = conv_cols * conv_term_t.shape[1]
+    conv_part, proj_part = halving_scatter(
+        [
+            stage[0, :conv_size].reshape(conv_cols, -1),
+            stage[0, conv_size:].reshape(proj_cols, -1),
+        ],
+        n_blk,
+    )
     conv_grad = conv_part.T
-    proj_grad = (
-        proj_part.reshape(-1)[:per_block]
-        .reshape(proj_term_t.shape[0] // n_dp, proj_term_t.shape[1] // n_blk)
-        .T
-    )
+    proj_grad = proj_part.T
     var_weight = jnp.exp(-log_var)
     lang_mean = loss_sum / jnp.maximum(counts, 1.0)
     loss = jnp.sum(var_weight * lang_mean + log_var)

time: 311 us -> 379 us (1.22); the launches traced: 310 us -> 374 us
  waiting for transfers between devices: 84.2 us -> 136 us
  other arithmetic: 25 us -> 45 us
  local copies, waits for them, and re-layouts: 32 us -> 21.6 us
    unnamed x2 -> x3, waiting for transfers between devices: 0.03 us -> 121 us
    reduce_scatter x1 -> x0, waiting for transfers between devices: 65.9 us -> none  [local(): stage = lax.psum_scatter(buf, 'dp', scatter_dimension=0, tiled=True)]
    convert_element_type x2, other arithmetic: 1.95 us -> 11.8 us  [halving_scatter(): p.reshape(p.shape[0], n_blk, -1).astype(jnp.float32)]
    concatenate x1, other arithmetic: 6.8 us -> 16.4 us  [scatter_buffer(): jnp.concatenate([conv_term_t.astype(jnp.bfloat16).reshape(n_dp, -1), proj...]
    reshape x5 -> x2, local copies, waits for them, and re-layouts: 14 us -> 7.09 us  [the longest x1 6.58 us: scatter_buffer(): conv_term_t.astype(jnp.bfloat16).reshape(n_dp, -1)]
  transfers between devices with their start and end apart: 10 -> 10, of which waited for: 7 -> 6; matrix products, arithmetic and copies ran while one was open for 4% -> 5% of each run, Pallas kernels for 0% -> 0%
where the time goes in v5:
time: 379 us; the launch traced here: 374 us
  waiting for transfers between devices  136 us (36%)
  blocking collectives  111 us (29%)
  other arithmetic  45 us (12%)
  matrix products  28.3 us (7%)
  local copies, waits for them, and re-layouts  21.6 us (6%)
  starting transfers between devices  18 us (5%)
  between operations  14.6 us (4%)
    unnamed x3, waiting for transfers between devices  121 us
    psum x1, blocking collectives, local(): counts = lax.psum(local_counts, ('blk', 'dp'))  80.2 us
    psum x1, blocking collectives, local(): loss_sum, scale_grad = lax.psum(batch_sums, 'dp')  30.3 us
    ppermute x8, starting transfers between devices, halving_scatter(): got = lax.ppermute(send.astype(jnp.bfloat16), 'blk', pairs)  17.9 us
    concatenate x1, other arithmetic, scatter_buffer(): jnp.concatenate([conv_term_t.astype(jnp.bfloat16).reshape(n_dp, -1), proj...  16.4 us
    ppermute x8, waiting for transfers between devices, halving_scatter(): got = lax.ppermute(send.astype(jnp.bfloat16), 'blk', pairs)  14.7 us
    convert_element_type x2, other arithmetic, halving_scatter(): p.reshape(p.shape[0], n_blk, -1).astype(jnp.float32)  11.8 us
    dot_general x1, matrix products, encode_back(): lax.dot_general(grad_pre, stacked, (((0,), (0,)), ((), ())), preferred_el...  9.34 us
  transfers between devices with their start and end apart: 10, of which 6 were waited for; matrix products, arithmetic and copies ran while one was open for 5% of the time, Pallas kernels for 0%

profile of v5, /device:TPU:8, one launch (start us, length us, event | category | flops | bytes accessed | tf_op | source)
XLA Modules:
  0.0 374.1 jit_solution(12851884227238241740)
XLA Ops:
  7.2 3.3 fusion.38
  10.6 0.9 concatenate.22
  12.2 3.3 copy-done.18
  15.5 9.3 %bitcast_reduce_fusion = (f32[64,1024]{1,0:T(8,128)S(1)}, f32[1024,1024]{1,0:T(8,128)}) fusion(bf16[3072,1024]{1,0:T(8,128)(2,1)S(1)} %copy-done.18, bf16[1024,1024]{1,0:T(8,128)(2,1)S(1)} %bitcast.90, bf16[1024,1024]{1,0:T(8,128)(2,1)S(1)} %bitcast.86, bf16[1024,1024]{1,0:T(8,128)(2,1)S(1)} %bitcast.88), kind=kOutput, calls=%fused_computation.17 | convolution fusion | flops 6470696960 | bytes 17039360 | tf_op jit(solution)/shard_map/dot_general | solution.py:22
  25.5 0.6 convert_reduce_fusion.1
  26.2 0.7 pad_maximum_fusion.4
  27.0 1.2 exp.20
  28.2 80.2 %psum.14 = f32[100]{0:T(128)S(1)} all-reduce(f32[100]{0:T(128)} %convert_reduce_fusion.1), channel_id=1, replica_groups=mesh['blk'=16,'dp'=16] {'blk','dp'}, use_global_device_ids=true, to_apply=%region_4.0 | all-reduce | flops 100 | bytes 800 | tf_op jit(solution)/shard_map/psum | solution.py:111
  108.4 1.2 maximum_divide_fusion
  109.6 1.2 convert_reduce_fusion
  110.8 0.9 select_reduce_fusion.5
  111.6 3.0 fusion.36
  114.6 2.6 select_reduce_fusion
  117.3 3.2 multiply_reduce_fusion
  120.6 2.4 multiply_reduce_fusion.2
  123.5 1.5 convolution_convert_fusion.1
  125.0 2.8 fusion.6
  127.8 9.3 %convolution_convert_fusion = bf16[1024,3072]{1,0:T(8,128)(2,1)} fusion(bf16[1024,1024]{1,0:T(8,128)(2,1)S(1)} %fusion.6, bf16[1024,1024]{1,0:T(8,128)(2,1)S(1)} %bitcast.91, bf16[1024,1024]{1,0:T(8,128)(2,1)S(1)} %bitcast.87, bf16[1024,1024]{1,0:T(8,128)(2,1)S(1)} %bitcast.89), kind=kOutput, calls=%fused_computation.6 | convolution fusion | flops 6464471040 | bytes 14680064 | tf_op jit(solution)/shard_map/dot_general | solution.py:55
  137.2 6.6 %reshape.131 = bf16[16,196608]{1,0:T(8,128)(2,1)} reshape(bf16[1024,3072]{1,0:T(8,128)(2,1)} %convolution_convert_fusion) | data formatting | bytes 12582912 | tf_op jit(solution)/shard_map/reshape | solution.py:64
  144.4 16.4 %pad_maximum_fusion = bf16[16,229376]{1,0:T(8,128)(2,1)} fusion(bf16[16,32768]{1,0:T(8,128)(2,1)S(1)} %reshape.132, bf16[16,196608]{1,0:T(8,128)(2,1)} %reshape.131), kind=kLoop, calls=%fused_computation | loop fusion | flops 14680064 | bytes 14680064 | tf_op jit(solution)/shard_map/concatenate | solution.py:62
  161.0 0.5 copy-done.20
  161.5 0.6 dynamic-slice.10
  162.1 30.3 %psum.15 = f32[2,100]{1,0:T(2,128)S(1)} all-reduce(f32[2,100]{1,0:T(2,128)S(1)} %pad_maximum_fusion.5), channel_id=1, replica_groups=mesh['blk'=16,'dp'=16] {'dp'}, use_global_device_ids=true, to_apply=%region_17.18 | all-reduce | flops 200 | bytes 1600 | tf_op jit(solution)/shard_map/psum | solution.py:165
  192.4 0.5 broadcast_subtract_fusion
  192.9 0.6 add_reduce_fusion
  193.5 0.5 slice_bitcast_fusion
  194.0 1.9 multiply_reduce_fusion.1
  195.9 0.8 divide_bitcast_fusion
  196.7 121.2 %all-reduce.5.cloned.1.call-done = bf16[16,229376]{1,0:T(8,128)(2,1)} async-done(((bf16[16,229376]{1,0:T(8,128)(2,1)}), bf16[16,229376]{1,0:T(8,128)(2,1)}) %all-reduce.5.cloned.1.call-update) | async-done | bytes 7340048
  317.9 2.2 fusion.21
  320.4 0.7 collective-permute-start.4
  321.0 9.6 %fusion.17 = f32[196608]{0:T(1024)S(1)} fusion(bf16[16,229376]{1,0:T(8,128)(2,1)} %all-reduce.5.cloned.1.call-done, u32[]{:T(128)} %bitcast.30), kind=kLoop, calls=%fused_computation.37 | loop fusion | flops 196608 | bytes 1179652 | tf_op jit(solution)/shard_map/convert_element_type | solution.py:73
  330.7 0.8 reshape.139
  331.5 0.5 dynamic-slice_convert_fusion.1
  332.2 1.6 collective-permute-start.5
  334.0 2.3 collective-permute-done.5
  336.3 2.6 collective-permute-start.6
  338.9 0.5 constant_dynamic-slice_fusion.5
  339.5 1.5 collective-permute-start
  341.1 4.9 %collective-permute-done = bf16[64,8,192]{2,1,0:T(8,128)(2,1)S(1)} collective-permute-done((bf16[64,8,192]{2,1,0:T(8,128)(2,1)S(1)}, bf16[64,8,192]{2,1,0:T(8,128)(2,1)S(1)}, u32[]{:S(2)}, u32[]{:S(2)}) %collective-permute-start) | collective-permute-done | bytes 196640 | tf_op jit(solution)/shard_map/ppermute | solution.py:83
  346.6 1.6 collective-permute-start.1
  348.5 3.8 %collective-permute-done.1 = bf16[64,4,192]{2,0,1:T(8,128)(2,1)S(1)} collective-permute-done((bf16[64,4,192]{2,0,1:T(8,128)(2,1)S(1)}, bf16[64,4,192]{2,0,1:T(8,128)(2,1)S(1)}, u32[]{:S(2)}, u32[]{:S(2)}) %collective-permute-start.1) | collective-permute-done | bytes 98336 | tf_op jit(solution)/shard_map/ppermute | solution.py:83
  352.6 5.5 %collective-permute-start.7 = (bf16[32,1,64]{2,0,1:T(8,128)(2,1)S(1)}, bf16[32,1,64]{2,0,1:T(8,128)(2,1)S(1)}, u32[]{:S(2)}, u32[]{:S(2)}) collective-permute-start(bf16[32,1,64]{2,0,1:T(8,128)(2,1)S(1)} %dynamic-slice_convert_fusion.7), channel_id=1, source_target_pairs={{0,128},{16,144},{32,160},{48,176},{64,192},{80,208},{96,224},{112... | collective-permute-start | bytes 12296 | tf_op jit(solution)/shard_map/ppermute | solution.py:83
  358.1 0.6 collective-permute-done.2
  358.7 4.1 %collective-permute-start.3 = (bf16[64,1,192]{2,0,1:T(8,128)(2,1)S(1)}, bf16[64,1,192]{2,0,1:T(8,128)(2,1)S(1)}, u32[]{:S(2)}, u32[]{:S(2)}) collective-permute-start(bf16[64,1,192]{2,0,1:T(8,128)(2,1)S(1)} %dynamic-slice_convert_fusion.5), channel_id=1, source_target_pairs={{0,128},{16,144},{32,160},{48,176},{64,192},{80,208},{96,224},{112... | collective-permute-start | bytes 73736 | tf_op jit(solution)/shard_map/ppermute | solution.py:83
  362.8 0.6 add_bitcast_fusion.1
  363.4 3.2 collective-permute-done.3
  366.6 0.6 add_bitcast_fusion
  (84 shorter events, 4.6 us)
Async XLA Ops:
  7.2 17.7 %copy-start = (bf16[1024,512]{1,0:T(8,128)(2,1)S(1)}, bf16[1024,512]{1,0:T(8,128)(2,1)}, u32[]{:S(2)}) copy-start(bf16[1024,512]{1,0:T(8,128)(2,1)} %param.10) | copy-start | bytes 3145732
  7.2 102.4 %all-gather.2.cloned.1.call-start = ((), (), s32[]{:S(2)}) async-start(), calls=%async_computation | async-start | bytes 2506752 | tf_op jit(solution)/shard_map/all_gather | solution.py:110
  10.6 1.6 copy-start.2
  10.6 4.9 %copy-start.18 = (bf16[3072,1024]{1,0:T(8,128)(2,1)S(1)}, bf16[3072,1024]{1,0:T(8,128)(2,1)}, u32[]{:S(2)}) copy-start(bf16[3072,1024]{1,0:T(8,128)(2,1)} %param.9) | copy-start | bytes 18874372
  11.5 13.4 %copy-start.6 = (bf16[64,16,1024]{2,1,0:T(8,128)(2,1)}, bf16[64,16,1024]{2,1,0:T(8,128)(2,1)S(1)}, u32[]{:S(2)}) copy-start(bf16[64,16,1024]{2,1,0:T(8,128)(2,1)S(1)} %concatenate.22) | copy-start | bytes 6291460
  11.9 13.0 %copy-start.8 = (bf16[64,16,1024]{2,1,0:T(8,128)(2,1)}, bf16[64,16,1024]{2,1,0:T(8,128)(2,1)S(1)}, u32[]{:S(2)}) copy-start(bf16[64,16,1024]{2,1,0:T(8,128)(2,1)S(1)} %concatenate.25) | copy-start | bytes 6291460
  15.5 9.8 %copy-start.10 = (bf16[1,64,512]{2,1,0:T(8,128)(2,1)S(1)}, bf16[1,64,512]{2,1,0:T(8,128)(2,1)}, u32[]{:S(2)}) copy-start(bf16[1,64,512]{2,1,0:T(8,128)(2,1)} %param.11) | copy-start | bytes 196612
  15.5 9.9 %copy-start.19 = (s32[1,64]{1,0:T(1,128)S(1)}, s32[1,64]{1,0:T(1,128)}, u32[]{:S(2)}) copy-start(s32[1,64]{1,0:T(1,128)} %param.12) | copy-start | bytes 772
  15.5 95.2 %copy-start.14 = (f32[100]{0:T(128)S(1)}, f32[100]{0:T(128)}, u32[]{:S(2)}) copy-start(f32[100]{0:T(128)} %param.14) | copy-start | bytes 1204
  25.3 84.3 %copy-start.12 = (f32[64]{0:T(128)}, f32[64]{0:T(128)S(1)}, u32[]{:S(2)}) copy-start(f32[64]{0:T(128)S(1)} %add_sqrt_fusion.1) | copy-start | bytes 772
  26.9 290.9 %all-reduce.5.cloned.1.call-start = ((), (), s32[]{:S(2)}) async-start(), calls=%async_computation.1 | async-start | bytes 14680064
  108.4 6.2 %copy-start.16 = (f32[100]{0:T(128)}, f32[100]{0:T(128)S(1)}, u32[]{:S(2)}) copy-start(f32[100]{0:T(128)S(1)} %psum.14) | copy-start | bytes 1204
  117.3 3.3 copy-start.13
  117.3 7.7 %copy-start.3 = (f32[1024,1024]{1,0:T(8,128)S(1)}, f32[1024,1024]{1,0:T(8,128)}, u32[]{:S(2)}) copy-start(f32[1024,1024]{1,0:T(8,128)} %get-tuple-element.34) | copy-start | bytes 12582916
  120.6 4.4 %copy-start.5 = (bf16[1024,1024]{1,0:T(8,128)(2,1)}, bf16[1024,1024]{1,0:T(8,128)(2,1)S(1)}, u32[]{:S(2)}) copy-start(bf16[1024,1024]{1,0:T(8,128)(2,1)S(1)} %get-tuple-element.30) | copy-start | bytes 6291460
  123.4 4.4 %copy-start.7 = (bf16[64,16,1024]{2,1,0:T(8,128)(2,1)S(1)}, bf16[64,16,1024]{2,1,0:T(8,128)(2,1)}, u32[]{:S(2)}) copy-start(bf16[64,16,1024]{2,1,0:T(8,128)(2,1)} %copy-done.6) | copy-start | bytes 6291460
  123.4 4.4 %copy-start.9 = (bf16[64,16,1024]{2,1,0:T(8,128)(2,1)S(1)}, bf16[64,16,1024]{2,1,0:T(8,128)(2,1)}, u32[]{:S(2)}) copy-start(bf16[64,16,1024]{2,1,0:T(8,128)(2,1)} %copy-done.8) | copy-start | bytes 6291460
  137.2 6.6 %copy-start.4 = (bf16[512,1024]{1,0:T(8,128)(2,1)S(1)}, bf16[512,1024]{1,0:T(8,128)(2,1)}, u32[]{:S(2)}) copy-start(bf16[512,1024]{1,0:T(8,128)(2,1)} %convolution_convert_fusion.1) | copy-start | bytes 3145732
  160.8 0.7 copy-start.20
  160.8 31.6 %copy-start.15 = (f32[100]{0:T(128)S(1)}, f32[100]{0:T(128)}, u32[]{:S(2)}) copy-start(f32[100]{0:T(128)} %param.15) | copy-start | bytes 1204
  160.8 31.6 %copy-start.17 = (f32[100]{0:T(128)S(1)}, f32[100]{0:T(128)}, u32[]{:S(2)}) copy-start(f32[100]{0:T(128)} %copy-done.16) | copy-start | bytes 1204
  160.8 33.2 %copy-start.11 = (bf16[1,64,512]{2,1,0:T(8,128)(2,1)S(1)}, bf16[1,64,512]{2,1,0:T(8,128)(2,1)}, u32[]{:S(2)}) copy-start(bf16[1,64,512]{2,1,0:T(8,128)(2,1)} %param.11) | copy-start | bytes 196612
  320.4 11.7 %collective-permute-start.4 = (bf16[32,8,64]{2,1,0:T(8,128)(2,1)S(1)}, bf16[32,8,64]{2,1,0:T(8,128)(2,1)S(1)}, u32[]{:S(2)}, u32[]{:S(2)}) collective-permute-start(bf16[32,8,64]{2,1,0:T(8,128)(2,1)S(1)} %bitcast.101), channel_id=1, source_target_pairs={{0,16},{16,0},{32,48},{48,32},{64,80},{80,64},{96,112},{112,96},{1... | collective-permute-start | bytes 98312 | tf_op jit(solution)/shard_map/ppermute | solution.py:83
  331.4 35.8 %copy-start.1 = (bf16[1024,512]{1,0:T(8,128)(2,1)S(1)}, bf16[1024,512]{1,0:T(8,128)(2,1)}, u32[]{:S(2)}) copy-start(bf16[1024,512]{1,0:T(8,128)(2,1)} %param.10) | copy-start | bytes 3145732
  332.2 4.0 %collective-permute-start.5 = (bf16[32,4,64]{2,0,1:T(8,128)(2,1)S(1)}, bf16[32,4,64]{2,0,1:T(8,128)(2,1)S(1)}, u32[]{:S(2)}, u32[]{:S(2)}) collective-permute-start(bf16[32,4,64]{2,0,1:T(8,128)(2,1)S(1)} %bitcast.102), channel_id=1, source_target_pairs={{0,32},{16,48},{32,0},{48,16},{64,96},{80,112},{96,64},{112,80},{1... | collective-permute-start | bytes 49160 | tf_op jit(solution)/shard_map/ppermute | solution.py:83
  336.3 4.8 %collective-permute-start.6 = (bf16[32,2,64]{2,0,1:T(8,128)(2,1)S(1)}, bf16[32,2,64]{2,0,1:T(8,128)(2,1)S(1)}, u32[]{:S(2)}, u32[]{:S(2)}) collective-permute-start(bf16[32,2,64]{2,0,1:T(8,128)(2,1)S(1)} %fusion.26), channel_id=1, source_target_pairs={{0,64},{16,80},{32,96},{48,112},{64,0},{80,16},{96,32},{112,48},{1... | collective-permute-start | bytes 24584 | tf_op jit(solution)/shard_map/ppermute | solution.py:83
  339.5 6.5 %collective-permute-start = (bf16[64,8,192]{2,1,0:T(8,128)(2,1)S(1)}, bf16[64,8,192]{2,1,0:T(8,128)(2,1)S(1)}, u32[]{:S(2)}, u32[]{:S(2)}) collective-permute-start(bf16[64,8,192]{2,1,0:T(8,128)(2,1)S(1)} %bitcast.97), channel_id=1, source_target_pairs={{0,16},{16,0},{32,48},{48,32},{64,80},{80,64},{96,112},{112,96},{1... | collective-permute-start | bytes 589832 | tf_op jit(solution)/shard_map/ppermute | solution.py:83
  346.6 5.6 %collective-permute-start.1 = (bf16[64,4,192]{2,0,1:T(8,128)(2,1)S(1)}, bf16[64,4,192]{2,0,1:T(8,128)(2,1)S(1)}, u32[]{:S(2)}, u32[]{:S(2)}) collective-permute-start(bf16[64,4,192]{2,0,1:T(8,128)(2,1)S(1)} %bitcast.100), channel_id=1, source_target_pairs={{0,32},{16,48},{32,0},{48,16},{64,96},{80,112},{96,64},{112,80},{1... | collective-permute-start | bytes 294920 | tf_op jit(solution)/shard_map/ppermute | solution.py:83
  352.4 6.3 %collective-permute-start.2 = (bf16[64,2,192]{2,0,1:T(8,128)(2,1)S(1)}, bf16[64,2,192]{2,0,1:T(8,128)(2,1)S(1)}, u32[]{:S(2)}, u32[]{:S(2)}) collective-permute-start(bf16[64,2,192]{2,0,1:T(8,128)(2,1)S(1)} %fusion.23), channel_id=1, source_target_pairs={{0,64},{16,80},{32,96},{48,112},{64,0},{80,16},{96,32},{112,48},{1... | collective-permute-start | bytes 147464 | tf_op jit(solution)/shard_map/ppermute | solution.py:83
  352.6 10.2 %collective-permute-start.7 = (bf16[32,1,64]{2,0,1:T(8,128)(2,1)S(1)}, bf16[32,1,64]{2,0,1:T(8,128)(2,1)S(1)}, u32[]{:S(2)}, u32[]{:S(2)}) collective-permute-start(bf16[32,1,64]{2,0,1:T(8,128)(2,1)S(1)} %dynamic-slice_convert_fusion.7), channel_id=1, source_target_pairs={{0,128},{16,144},{32,160},{48,176},{64,192},{80,208},{96,224},{112... | collective-permute-start | bytes 12296 | tf_op jit(solution)/shard_map/ppermute | solution.py:83
  358.7 7.9 %collective-permute-start.3 = (bf16[64,1,192]{2,0,1:T(8,128)(2,1)S(1)}, bf16[64,1,192]{2,0,1:T(8,128)(2,1)S(1)}, u32[]{:S(2)}, u32[]{:S(2)}) collective-permute-start(bf16[64,1,192]{2,0,1:T(8,128)(2,1)S(1)} %dynamic-slice_convert_fusion.5), channel_id=1, source_target_pairs={{0,128},{16,144},{32,160},{48,176},{64,192},{80,208},{96,224},{112... | collective-permute-start | bytes 73736 | tf_op jit(solution)/shard_map/ppermute | solution.py:83
Sparse Core Ops, SparseCore 0:
  27.1 77.5 all-gather.1
  161.0 156.8 all-reduce.4

commit v6 on v5

--- a/solution.py
+++ b/solution.py
@@ -34,13 +34,18 @@
     return (text_float / text_len, text_len)
 
 
-def encode_back(stacked, preact, pooled, audio_unit, audio_len, grad_audio, proj_weight):
+def encode_back(stacked, preact, pooled, audio_unit, audio_len, grad_audio, proj_weight, n_blk):
     clips = pooled.shape[0]
     steps_count = preact.shape[0] // clips
     radial = jnp.sum(audio_unit * grad_audio, axis=-1, keepdims=True)
     grad_embed = ((grad_audio - audio_unit * radial) / audio_len).astype(jnp.bfloat16)
+    width = pooled.shape[1]
+    pooled_perm = pooled.reshape(clips, n_blk, 2, width // n_blk // 2).transpose(0, 2, 1, 3)
     proj_term_t = lax.dot_general(
-        grad_embed, pooled, (((0,), (0,)), ((), ())), preferred_element_type=jnp.float32
+        grad_embed,
+        pooled_perm.reshape(clips, width),
+        (((0,), (0,)), ((), ())),
+        preferred_element_type=jnp.float32,
     )
     grad_pooled = (
         lax.dot_general(
@@ -59,13 +64,10 @@
 
 
 def scatter_buffer(conv_term_t, proj_term_t, n_dp):
-    return jnp.concatenate(
-        [
-            conv_term_t.astype(jnp.bfloat16).reshape(n_dp, -1),
-            proj_term_t.astype(jnp.bfloat16).reshape(n_dp, -1),
-        ],
-        axis=1,
-    )
+    conv_part = conv_term_t.astype(jnp.bfloat16).reshape(n_dp, -1, conv_term_t.shape[1])
+    rows = conv_part.shape[1]
+    proj_part = proj_term_t.astype(jnp.bfloat16).reshape(n_dp, rows, -1)
+    return jnp.concatenate([conv_part, proj_part], axis=2)
 
 
 def halving_scatter(parts, n_blk):
@@ -157,24 +159,21 @@
         ]
     )
     conv_term_t, proj_term_t = encode_back(
-        stacked, preact, pooled, audio_unit, audio_len, grad_audio, proj_weight
+        stacked, preact, pooled, audio_unit, audio_len, grad_audio, proj_weight, n_blk
     )
     buf = scatter_buffer(conv_term_t, proj_term_t, n_dp)
     buf, batch_sums = lax.optimization_barrier((buf, batch_sums))
     stage = lax.psum_scatter(buf, "dp", scatter_dimension=0, tiled=True)
     loss_sum, scale_grad = lax.psum(batch_sums, "dp")
-    conv_cols = conv_term_t.shape[0] // n_dp
+    conv_width = conv_term_t.shape[1]
+    conv_part, proj_part = halving_scatter(
+        [stage[0, :, :conv_width], stage[0, :, conv_width:]], n_blk
+    )
+    conv_grad = conv_part.T
     proj_cols = proj_term_t.shape[0] // n_dp
-    conv_size = conv_cols * conv_term_t.shape[1]
-    conv_part, proj_part = halving_scatter(
-        [
-            stage[0, :conv_size].reshape(conv_cols, -1),
-            stage[0, conv_size:].reshape(proj_cols, -1),
-        ],
-        n_blk,
-    )
-    conv_grad = conv_part.T
-    proj_grad = proj_part.T
+    proj_grad = (
+        proj_part.reshape(proj_cols, 2, -1).transpose(1, 2, 0).reshape(-1, proj_cols)
+    )
     var_weight = jnp.exp(-log_var)
     lang_mean = loss_sum / jnp.maximum(counts, 1.0)
     loss = jnp.sum(var_weight * lang_mean + log_var)

time: 379 us -> 289 us (0.76); the launches traced: 374 us -> 289 us
  waiting for transfers between devices: 136 us -> 78.7 us
  other arithmetic: 45 us -> 23.9 us
  local copies, waits for them, and re-layouts: 21.6 us -> 15.8 us
    unnamed x3 -> x2, waiting for transfers between devices: 121 us -> 0.03 us
    reduce_scatter x0 -> x1, waiting for transfers between devices: none -> 63.4 us  [local(): stage = lax.psum_scatter(buf, 'dp', scatter_dimension=0, tiled=True)]
    concatenate x1, other arithmetic: 16.4 us -> 6.36 us  [scatter_buffer(): return jnp.concatenate([conv_part, proj_part], axis=2)]
    convert_element_type x2, other arithmetic: 11.8 us -> 1.9 us  [halving_scatter(): p.reshape(p.shape[0], n_blk, -1).astype(jnp.float32)]
    reshape x2, local copies, waits for them, and re-layouts: 7.09 us -> 1.31 us  [the longest x1 0.7 us: local(): proj_part.reshape(proj_cols, 2, -1).transpose(1, 2, 0)]
  transfers between devices with their start and end apart: 10 -> 10, of which waited for: 6 -> 7; matrix products, arithmetic and copies ran while one was open for 5% -> 4% of each run, Pallas kernels for 0% -> 0%
where the time goes in v6:
time: 289 us
  blocking collectives  110 us (38%)
  waiting for transfers between devices  78.7 us (27%)
  matrix products  27.4 us (9%)
  other arithmetic  23.9 us (8%)
  starting transfers between devices  17.9 us (6%)
  local copies, waits for them, and re-layouts  15.8 us (5%)
  between operations  14.6 us (5%)
    psum x1, blocking collectives, local(): counts = lax.psum(local_counts, ('blk', 'dp'))  79.7 us
    reduce_scatter x1, waiting for transfers between devices, local(): stage = lax.psum_scatter(buf, 'dp', scatter_dimension=0, tiled=True)  63.4 us
    psum x1, blocking collectives, local(): loss_sum, scale_grad = lax.psum(batch_sums, 'dp')  30.7 us
    ppermute x8, starting transfers between devices, halving_scatter(): got = lax.ppermute(send.astype(jnp.bfloat16), 'blk', pairs)  17.8 us
    ppermute x8, waiting for transfers between devices, halving_scatter(): got = lax.ppermute(send.astype(jnp.bfloat16), 'blk', pairs)  15.3 us
    dot_general x1, matrix products, encode_back(): lax.dot_general(grad_pre, stacked, (((0,), (0,)), ((), ())), preferred_el...  9.38 us
    dot_general x1, matrix products, encode(): preact = jnp.dot(stacked, conv_weight, preferred_element_type=jnp.float32)  9.35 us
    concatenate x1, other arithmetic, scatter_buffer(): return jnp.concatenate([conv_part, proj_part], axis=2)  6.36 us
  transfers between devices with their start and end apart: 10, of which 7 were waited for; matrix products, arithmetic and copies ran while one was open for 4% of the time, Pallas kernels for 0%

profile of v6, /device:TPU:8, one launch (start us, length us, event | category | flops | bytes accessed | tf_op | source)
XLA Modules:
  0.0 288.6 jit_solution(16766312715072271520)
XLA Ops:
  7.2 3.3 %fusion.34 = (bf16[64,15,1024]{2,1,0:T(8,128)(2,1)S(1)}, bf16[64,15,1024]{2,1,0:T(8,128)(2,1)S(1)}) fusion(bf16[64,16,1024]{2,1,0:T(8,128)(2,1)} %bitcast.92), kind=kLoop, calls=%fused_computation.106 | loop fusion | bytes 7864320 | tf_op jit(solution)/shard_map/slice | solution.py:12
  10.6 0.9 concatenate.22
  12.2 3.3 %copy-done.17 = bf16[3072,1024]{1,0:T(8,128)(2,1)S(1)} copy-done((bf16[3072,1024]{1,0:T(8,128)(2,1)S(1)}, bf16[3072,1024]{1,0:T(8,128)(2,1)}, u32[]{:S(2)}) %copy-start.17) | copy-done | bytes 6291480
  15.5 9.3 %bitcast_reduce_fusion = (f32[64,1024]{1,0:T(8,128)S(1)}, f32[1024,1024]{1,0:T(8,128)}) fusion(bf16[3072,1024]{1,0:T(8,128)(2,1)S(1)} %copy-done.17, bf16[1024,1024]{1,0:T(8,128)(2,1)S(1)} %bitcast.98, bf16[1024,1024]{1,0:T(8,128)(2,1)S(1)} %bitcast.93, bf16[1024,1024]{1,0:T(8,128)(2,1)S(1)} %bitcast.96), kind=kOutput, calls=%fused_computation.17 | convolution fusion | flops 6470696960 | bytes 17039360 | tf_op jit(solution)/shard_map/dot_general | solution.py:22
  25.5 0.6 convert_reduce_fusion.1
  26.3 0.7 pad_maximum_fusion.4
  27.0 0.8 copy.42
  28.4 1.0 copy.43
  29.4 79.7 %psum.14 = f32[100]{0:T(128)S(1)} all-reduce(f32[100]{0:T(128)} %convert_reduce_fusion.1), channel_id=1, replica_groups=mesh['blk'=16,'dp'=16] {'blk','dp'}, use_global_device_ids=true, to_apply=%region_4.0 | all-reduce | flops 100 | bytes 800 | tf_op jit(solution)/shard_map/psum | solution.py:113
  109.0 0.5 maximum_divide_fusion
  109.5 1.2 convert_reduce_fusion
  110.7 0.9 select_reduce_fusion.5
  111.6 3.0 %fusion.32 = (f32[1024]{0:T(1024)S(1)}, f32[1024]{0:T(1024)S(1)}, f32[1024,1024]{1,0:T(8,128)S(1)}) fusion(f32[1024]{0:T(1024)S(1)} %get-tuple-element.22, bf16[1024,1152]{1,0:T(8,128)(2,1)} %all-gather.2.cloned.1.call-done, f32[1024]{0:T(1024)S(1)} %get-tuple-element.23), kind=kOutput, calls=%fused_computation.105 | convolution fusion | flops 1077934080 | bytes 6307840 | tf_op jit(solution)/shard_map/dot_general | solution.py:125
  114.6 2.6 select_reduce_fusion
  117.3 3.2 %multiply_reduce_fusion = (f32[1024]{0:T(1024)S(1)}, bf16[1024,1024]{1,0:T(8,128)(2,1)S(1)}) fusion(f32[1024,1024]{1,0:T(8,128)S(1)} %get-tuple-element.37, f32[1024]{0:T(1024)S(1)} %get-tuple-element.28, f32[1024]{0:T(1024)S(1)} %get-tuple-element.21, f32[1024]{0:T(1024)S(1)} %get-tuple-element.27, f32[1024]{0:T(1024)S(1)} %get-tuple-element.22, ...), kind=kLoop, calls=%fused_computation.18 | loop fusion | flops 14679040 | bytes 6316032 | tf_op jit(solution)/shard_map/reduce_sum | solution.py:143
  120.5 2.4 multiply_reduce_fusion.2
  123.4 2.8 fusion.6
  126.3 9.4 %convolution_convert_fusion = bf16[1024,3072]{1,0:T(8,128)(2,1)} fusion(bf16[1024,1024]{1,0:T(8,128)(2,1)S(1)} %fusion.6, bf16[1024,1024]{1,0:T(8,128)(2,1)S(1)} %bitcast.99, bf16[1024,1024]{1,0:T(8,128)(2,1)S(1)} %bitcast.94, bf16[1024,1024]{1,0:T(8,128)(2,1)S(1)} %bitcast.97), kind=kOutput, calls=%fused_computation.6 | convolution fusion | flops 6464471040 | bytes 14680064 | tf_op jit(solution)/shard_map/dot_general | solution.py:60
  135.7 0.6 convolution_convert_fusion.1
  136.2 0.6 reshape.144
  137.0 6.4 %pad_maximum_fusion = bf16[16,64,3584]{2,1,0:T(8,128)(2,1)} fusion(bf16[16,64,512]{2,1,0:T(8,128)(2,1)S(1)} %reshape.144, bf16[16,64,3072]{2,1,0:T(8,128)(2,1)} %bitcast.95), kind=kLoop, calls=%fused_computation | loop fusion | flops 14680064 | bytes 14680064 | tf_op jit(solution)/shard_map/concatenate | solution.py:70
  143.5 30.7 %psum.15 = f32[2,100]{1,0:T(2,128)S(1)} all-reduce(f32[2,100]{1,0:T(2,128)S(1)} %pad_maximum_fusion.5), channel_id=1, replica_groups=mesh['blk'=16,'dp'=16] {'dp'}, use_global_device_ids=true, to_apply=%region_17.18 | all-reduce | flops 200 | bytes 1600 | tf_op jit(solution)/shard_map/psum | solution.py:167
  174.2 0.5 broadcast_subtract_fusion
  174.8 0.6 add_reduce_fusion
  175.9 1.9 multiply_reduce_fusion.1
  177.7 0.8 divide_bitcast_fusion
  178.5 63.4 %reduce-scatter.2.cloned.1.call-done = bf16[1,64,3584]{2,1,0:T(8,128)(2,1)} async-done(((bf16[16,64,3584]{2,1,0:T(8,128)(2,1)}), bf16[1,64,3584]{2,1,0:T(8,128)(2,1)}) %reduce-scatter.2.cloned.1.call-update) | async-done | bytes 458768 | tf_op jit(solution)/shard_map/reduce_scatter | solution.py:166
  241.9 0.8 slice_convert_fusion.1
  242.9 0.7 collective-permute-start.4
  243.6 1.0 slice_convert_fusion
  244.6 1.0 reshape.152
  245.6 1.6 collective-permute-done.4
  247.3 1.6 collective-permute-start.5
  248.9 0.5 dynamic-slice_convert_fusion
  249.5 2.0 collective-permute-done.5
  251.5 2.4 collective-permute-start.6
  253.9 0.5 constant_dynamic-slice_fusion.2
  254.5 0.7 collective-permute-start
  255.2 1.0 collective-permute-done.6
  256.2 4.8 %collective-permute-done = bf16[64,8,192]{2,1,0:T(8,128)(2,1)S(1)} collective-permute-done((bf16[64,8,192]{2,1,0:T(8,128)(2,1)S(1)}, bf16[64,8,192]{2,1,0:T(8,128)(2,1)S(1)}, u32[]{:S(2)}, u32[]{:S(2)}) %collective-permute-start) | collective-permute-done | bytes 196640 | tf_op jit(solution)/shard_map/ppermute | solution.py:85
  261.7 1.8 collective-permute-start.1
  263.7 3.0 %collective-permute-done.1 = bf16[64,4,192]{2,0,1:T(8,128)(2,1)S(1)} collective-permute-done((bf16[64,4,192]{2,0,1:T(8,128)(2,1)S(1)}, bf16[64,4,192]{2,0,1:T(8,128)(2,1)S(1)}, u32[]{:S(2)}, u32[]{:S(2)}) %collective-permute-start.1) | collective-permute-done | bytes 98336 | tf_op jit(solution)/shard_map/ppermute | solution.py:85
  266.8 1.3 collective-permute-start.2
  268.2 5.0 %collective-permute-start.7 = (bf16[64,1,32]{0,2,1:T(8,128)(2,1)S(1)}, bf16[64,1,32]{0,2,1:T(8,128)(2,1)S(1)}, u32[]{:S(2)}, u32[]{:S(2)}) collective-permute-start(bf16[64,1,32]{0,2,1:T(8,128)(2,1)S(1)} %dynamic-slice_convert_fusion.6), channel_id=1, source_target_pairs={{0,128},{16,144},{32,160},{48,176},{64,192},{80,208},{96,224},{112... | collective-permute-start | bytes 12296 | tf_op jit(solution)/shard_map/ppermute | solution.py:85
  273.2 4.3 %collective-permute-start.3 = (bf16[64,1,192]{2,0,1:T(8,128)(2,1)S(1)}, bf16[64,1,192]{2,0,1:T(8,128)(2,1)S(1)}, u32[]{:S(2)}, u32[]{:S(2)}) collective-permute-start(bf16[64,1,192]{2,0,1:T(8,128)(2,1)S(1)} %dynamic-slice_convert_fusion.4), channel_id=1, source_target_pairs={{0,128},{16,144},{32,160},{48,176},{64,192},{80,208},{96,224},{112... | collective-permute-start | bytes 73736 | tf_op jit(solution)/shard_map/ppermute | solution.py:85
  277.6 0.7 reshape.149
  278.3 2.8 collective-permute-done.3
  281.1 0.6 add_bitcast_fusion
  (81 shorter events, 4.6 us)
Async XLA Ops:
  7.2 17.8 %copy-start = (bf16[1024,512]{1,0:T(8,128)(2,1)S(1)}, bf16[1024,512]{1,0:T(8,128)(2,1)}, u32[]{:S(2)}) copy-start(bf16[1024,512]{1,0:T(8,128)(2,1)} %param.10) | copy-start | bytes 3145732
  7.2 102.4 %all-gather.2.cloned.1.call-start = ((), (), s32[]{:S(2)}) async-start(), calls=%async_computation.1 | async-start | bytes 2506752 | tf_op jit(solution)/shard_map/all_gather | solution.py:112
  10.6 1.6 copy-start.1
  10.6 4.9 %copy-start.17 = (bf16[3072,1024]{1,0:T(8,128)(2,1)S(1)}, bf16[3072,1024]{1,0:T(8,128)(2,1)}, u32[]{:S(2)}) copy-start(bf16[3072,1024]{1,0:T(8,128)(2,1)} %param.9) | copy-start | bytes 18874372
  11.5 13.4 %copy-start.4 = (bf16[64,16,1024]{2,1,0:T(8,128)(2,1)}, bf16[64,16,1024]{2,1,0:T(8,128)(2,1)S(1)}, u32[]{:S(2)}) copy-start(bf16[64,16,1024]{2,1,0:T(8,128)(2,1)S(1)} %concatenate.22) | copy-start | bytes 6291460
  11.9 13.0 %copy-start.6 = (bf16[64,16,1024]{2,1,0:T(8,128)(2,1)}, bf16[64,16,1024]{2,1,0:T(8,128)(2,1)S(1)}, u32[]{:S(2)}) copy-start(bf16[64,16,1024]{2,1,0:T(8,128)(2,1)S(1)} %concatenate.25) | copy-start | bytes 6291460
  15.5 9.8 %copy-start.8 = (bf16[1,64,512]{2,1,0:T(8,128)(2,1)S(1)}, bf16[1,64,512]{2,1,0:T(8,128)(2,1)}, u32[]{:S(2)}) copy-start(bf16[1,64,512]{2,1,0:T(8,128)(2,1)} %param.11) | copy-start | bytes 196612
  15.5 10.0 %copy-start.18 = (s32[1,64]{1,0:T(1,128)S(1)}, s32[1,64]{1,0:T(1,128)}, u32[]{:S(2)}) copy-start(s32[1,64]{1,0:T(1,128)} %param.12) | copy-start | bytes 772
  15.5 12.4 %copy-start.19 = (f32[100]{0:T(128)S(1)}, f32[100]{0:T(128)}, u32[]{:S(2)}) copy-start(f32[100]{0:T(128)} %param.13) | copy-start | bytes 1204
  15.5 93.5 %copy-start.13 = (f32[100]{0:T(128)S(1)}, f32[100]{0:T(128)}, u32[]{:S(2)}) copy-start(f32[100]{0:T(128)} %param.15) | copy-start | bytes 1204
  15.5 95.2 %copy-start.12 = (f32[100]{0:T(128)S(1)}, f32[100]{0:T(128)}, u32[]{:S(2)}) copy-start(f32[100]{0:T(128)} %param.14) | copy-start | bytes 1204
  25.3 3.0 %copy-start.10 = (f32[64]{0:T(128)}, f32[64]{0:T(128)S(1)}, u32[]{:S(2)}) copy-start(f32[64]{0:T(128)S(1)} %add_sqrt_fusion.1) | copy-start | bytes 772
  27.0 214.9 %reduce-scatter.2.cloned.1.call-start = ((), (), s32[]{:S(2)}) async-start(), calls=%async_computation.2 | async-start | bytes 7798784 | tf_op jit(solution)/shard_map/reduce_scatter | solution.py:166
  109.0 5.6 %copy-start.15 = (f32[100]{0:T(128)}, f32[100]{0:T(128)S(1)}, u32[]{:S(2)}) copy-start(f32[100]{0:T(128)S(1)} %psum.14) | copy-start | bytes 1204
  117.2 3.3 %copy-start.11 = (f32[64]{0:T(128)S(1)}, f32[64]{0:T(128)}, u32[]{:S(2)}) copy-start(f32[64]{0:T(128)} %copy-done.10) | copy-start | bytes 772
  117.3 6.1 %copy-start.2 = (f32[1024,1024]{1,0:T(8,128)S(1)}, f32[1024,1024]{1,0:T(8,128)}, u32[]{:S(2)}) copy-start(f32[1024,1024]{1,0:T(8,128)} %get-tuple-element.34) | copy-start | bytes 12582916
  120.5 2.9 %copy-start.3 = (bf16[1024,1024]{1,0:T(8,128)(2,1)}, bf16[1024,1024]{1,0:T(8,128)(2,1)S(1)}, u32[]{:S(2)}) copy-start(bf16[1024,1024]{1,0:T(8,128)(2,1)S(1)} %get-tuple-element.30) | copy-start | bytes 6291460
  122.9 3.3 %copy-start.5 = (bf16[64,16,1024]{2,1,0:T(8,128)(2,1)S(1)}, bf16[64,16,1024]{2,1,0:T(8,128)(2,1)}, u32[]{:S(2)}) copy-start(bf16[64,16,1024]{2,1,0:T(8,128)(2,1)} %copy-done.4) | copy-start | bytes 6291460
  122.9 3.3 %copy-start.7 = (bf16[64,16,1024]{2,1,0:T(8,128)(2,1)S(1)}, bf16[64,16,1024]{2,1,0:T(8,128)(2,1)}, u32[]{:S(2)}) copy-start(bf16[64,16,1024]{2,1,0:T(8,128)(2,1)} %copy-done.6) | copy-start | bytes 6291460
  143.4 30.9 %copy-start.14 = (f32[100]{0:T(128)S(1)}, f32[100]{0:T(128)}, u32[]{:S(2)}) copy-start(f32[100]{0:T(128)} %param.15) | copy-start | bytes 1204
  143.4 30.9 %copy-start.16 = (f32[100]{0:T(128)S(1)}, f32[100]{0:T(128)}, u32[]{:S(2)}) copy-start(f32[100]{0:T(128)} %copy-done.15) | copy-start | bytes 1204
  143.4 32.5 %copy-start.9 = (bf16[1,64,512]{2,1,0:T(8,128)(2,1)S(1)}, bf16[1,64,512]{2,1,0:T(8,128)(2,1)}, u32[]{:S(2)}) copy-start(bf16[1,64,512]{2,1,0:T(8,128)(2,1)} %param.11) | copy-start | bytes 196612
  242.9 4.4 %collective-permute-start.4 = (bf16[64,8,32]{0,2,1:T(8,128)(2,1)S(1)}, bf16[64,8,32]{0,2,1:T(8,128)(2,1)S(1)}, u32[]{:S(2)}, u32[]{:S(2)}) collective-permute-start(bf16[64,8,32]{0,2,1:T(8,128)(2,1)S(1)} %fusion.22), channel_id=1, source_target_pairs={{0,16},{16,0},{32,48},{48,32},{64,80},{80,64},{96,112},{112,96},{1... | collective-permute-start | bytes 98312 | tf_op jit(solution)/shard_map/ppermute | solution.py:85
  247.3 4.2 %collective-permute-start.5 = (bf16[64,4,32]{0,2,1:T(8,128)(2,1)S(1)}, bf16[64,4,32]{0,2,1:T(8,128)(2,1)S(1)}, u32[]{:S(2)}, u32[]{:S(2)}) collective-permute-start(bf16[64,4,32]{0,2,1:T(8,128)(2,1)S(1)} %fusion.23), channel_id=1, source_target_pairs={{0,32},{16,48},{32,0},{48,16},{64,96},{80,112},{96,64},{112,80},{1... | collective-permute-start | bytes 49160 | tf_op jit(solution)/shard_map/ppermute | solution.py:85
  251.5 4.7 %collective-permute-start.6 = (bf16[64,2,32]{0,2,1:T(8,128)(2,1)S(1)}, bf16[64,2,32]{0,2,1:T(8,128)(2,1)S(1)}, u32[]{:S(2)}, u32[]{:S(2)}) collective-permute-start(bf16[64,2,32]{0,2,1:T(8,128)(2,1)S(1)} %fusion.24), channel_id=1, source_target_pairs={{0,64},{16,80},{32,96},{48,112},{64,0},{80,16},{96,32},{112,48},{1... | collective-permute-start | bytes 24584 | tf_op jit(solution)/shard_map/ppermute | solution.py:85
  254.5 6.5 %collective-permute-start = (bf16[64,8,192]{2,1,0:T(8,128)(2,1)S(1)}, bf16[64,8,192]{2,1,0:T(8,128)(2,1)S(1)}, u32[]{:S(2)}, u32[]{:S(2)}) collective-permute-start(bf16[64,8,192]{2,1,0:T(8,128)(2,1)S(1)} %bitcast.108), channel_id=1, source_target_pairs={{0,16},{16,0},{32,48},{48,32},{64,80},{80,64},{96,112},{112,96},{1... | collective-permute-start | bytes 589832 | tf_op jit(solution)/shard_map/ppermute | solution.py:85
  261.7 5.1 %collective-permute-start.1 = (bf16[64,4,192]{2,0,1:T(8,128)(2,1)S(1)}, bf16[64,4,192]{2,0,1:T(8,128)(2,1)S(1)}, u32[]{:S(2)}, u32[]{:S(2)}) collective-permute-start(bf16[64,4,192]{2,0,1:T(8,128)(2,1)S(1)} %bitcast.111), channel_id=1, source_target_pairs={{0,32},{16,48},{32,0},{48,16},{64,96},{80,112},{96,64},{112,80},{1... | collective-permute-start | bytes 294920 | tf_op jit(solution)/shard_map/ppermute | solution.py:85
  266.8 6.3 %collective-permute-start.2 = (bf16[64,2,192]{2,0,1:T(8,128)(2,1)S(1)}, bf16[64,2,192]{2,0,1:T(8,128)(2,1)S(1)}, u32[]{:S(2)}, u32[]{:S(2)}) collective-permute-start(bf16[64,2,192]{2,0,1:T(8,128)(2,1)S(1)} %fusion.21), channel_id=1, source_target_pairs={{0,64},{16,80},{32,96},{48,112},{64,0},{80,16},{96,32},{112,48},{1... | collective-permute-start | bytes 147464 | tf_op jit(solution)/shard_map/ppermute | solution.py:85
  268.2 9.3 %collective-permute-start.7 = (bf16[64,1,32]{0,2,1:T(8,128)(2,1)S(1)}, bf16[64,1,32]{0,2,1:T(8,128)(2,1)S(1)}, u32[]{:S(2)}, u32[]{:S(2)}) collective-permute-start(bf16[64,1,32]{0,2,1:T(8,128)(2,1)S(1)} %dynamic-slice_convert_fusion.6), channel_id=1, source_target_pairs={{0,128},{16,144},{32,160},{48,176},{64,192},{80,208},{96,224},{112... | collective-permute-start | bytes 12296 | tf_op jit(solution)/shard_map/ppermute | solution.py:85
  273.2 7.9 %collective-permute-start.3 = (bf16[64,1,192]{2,0,1:T(8,128)(2,1)S(1)}, bf16[64,1,192]{2,0,1:T(8,128)(2,1)S(1)}, u32[]{:S(2)}, u32[]{:S(2)}) collective-permute-start(bf16[64,1,192]{2,0,1:T(8,128)(2,1)S(1)} %dynamic-slice_convert_fusion.4), channel_id=1, source_target_pairs={{0,128},{16,144},{32,160},{48,176},{64,192},{80,208},{96,224},{112... | collective-permute-start | bytes 73736 | tf_op jit(solution)/shard_map/ppermute | solution.py:85
Sparse Core Ops, SparseCore 0:
  27.1 76.7 all-gather.1
  143.5 98.3 reduce-scatter.1

commit v7 on v6

--- a/solution.py
+++ b/solution.py
@@ -72,7 +72,12 @@
 
 def halving_scatter(parts, n_blk):
     me = lax.axis_index("blk")
-    parts = [p.reshape(p.shape[0], n_blk, -1).astype(jnp.float32) for p in parts]
+    segs = [p.shape[1] // n_blk for p in parts]
+    parts = [
+        jnp.concatenate(
+            [p.reshape(p.shape[0], n_blk, -1) for p in parts], axis=2
+        ).astype(jnp.float32)
+    ]
     bit = 1
     while bit < n_blk:
         mine = (me // bit) % 2
@@ -86,7 +91,8 @@
             kept.append(keep + got.astype(jnp.float32))
         parts = kept
         bit *= 2
-    return [p[:, 0, :] for p in parts]
+    joined = parts[0][:, 0, :]
+    return [joined[:, : segs[0]], joined[:, segs[0] :]]
 
 
 def local(

time: 289 us -> 340 us (1.18)
  waiting for transfers between devices: 78.7 us -> 115 us
  local copies, waits for them, and re-layouts: 15.8 us -> 30.2 us
  other arithmetic: 23.9 us -> 29.8 us
  starting transfers between devices: 17.9 us -> 12.3 us
    reduce_scatter x1, waiting for transfers between devices: 63.4 us -> 103 us  [local(): stage = lax.psum_scatter(buf, 'dp', scatter_dimension=0, tiled=True)]
    reshape x0 -> x1, local copies, waits for them, and re-layouts: none -> 12.1 us  [scatter_buffer(): conv_term_t.astype(jnp.bfloat16).reshape(n_dp, -1, conv_term_t.shape[1])]
    concatenate x1, other arithmetic: 6.36 us -> 14.7 us  [scatter_buffer(): return jnp.concatenate([conv_part, proj_part], axis=2)]
    ppermute x8 -> x4, starting transfers between devices: 17.8 us -> 12.2 us  [halving_scatter(): got = lax.ppermute(send.astype(jnp.bfloat16), 'blk', pairs)]
    ppermute x8 -> x4, waiting for transfers between devices: 15.3 us -> 11.9 us  [halving_scatter(): got = lax.ppermute(send.astype(jnp.bfloat16), 'blk', pairs)]
  transfers between devices with their start and end apart: 10 -> 6, of which waited for: 7 -> 5; matrix products, arithmetic and copies ran while one was open for 4% -> 2% of each run, Pallas kernels for 0% -> 0%
where the time goes in v7:
time: 340 us; the launch traced here: 339 us
  waiting for transfers between devices  115 us (34%)
  blocking collectives  110 us (32%)
  local copies, waits for them, and re-layouts  30.2 us (9%)
  other arithmetic  29.8 us (9%)
  matrix products  27.3 us (8%)
  between operations  14.6 us (4%)
  starting transfers between devices  12.3 us (4%)
    reduce_scatter x1, waiting for transfers between devices, local(): stage = lax.psum_scatter(buf, 'dp', scatter_dimension=0, tiled=True)  103 us
    psum x1, blocking collectives, local(): counts = lax.psum(local_counts, ('blk', 'dp'))  79.8 us
    psum x1, blocking collectives, local(): loss_sum, scale_grad = lax.psum(batch_sums, 'dp')  30.3 us
    concatenate x1, other arithmetic, scatter_buffer(): return jnp.concatenate([conv_part, proj_part], axis=2)  14.7 us
    ppermute x4, starting transfers between devices, halving_scatter(): got = lax.ppermute(send.astype(jnp.bfloat16), 'blk', pairs)  12.2 us
    reshape x1, local copies, waits for them, and re-layouts, scatter_buffer(): conv_term_t.astype(jnp.bfloat16).reshape(n_dp, -1, conv_term_t.shape[1])  12.1 us
    ppermute x4, waiting for transfers between devices, halving_scatter(): got = lax.ppermute(send.astype(jnp.bfloat16), 'blk', pairs)  11.9 us
    dot_general x1, matrix products, encode(): preact = jnp.dot(stacked, conv_weight, preferred_element_type=jnp.float32)  9.35 us
  transfers between devices with their start and end apart: 6, of which 5 were waited for; matrix products, arithmetic and copies ran while one was open for 2% of the time, Pallas kernels for 0%

profile of v7, /device:TPU:8, one launch (start us, length us, event | category | flops | bytes accessed | tf_op | source)
XLA Modules:
  0.0 339.3 jit_solution(15330037054570349292)
XLA Ops:
  7.2 3.3 fusion.32
  10.6 0.9 concatenate.30
  11.5 0.4 concatenate.33
  12.2 3.3 copy-done.23
  15.5 9.3 %bitcast_reduce_fusion = (f32[64,1024]{1,0:T(8,128)S(1)}, f32[1024,1024]{1,0:T(8,128)}) fusion(bf16[3072,1024]{1,0:T(8,128)(2,1)S(1)} %copy-done.23, bf16[1024,1024]{1,0:T(8,128)(2,1)S(1)} %bitcast.85, bf16[1024,1024]{1,0:T(8,128)(2,1)S(1)} %bitcast.79, bf16[1024,1024]{1,0:T(8,128)(2,1)S(1)} %bitcast.83), kind=kOutput, calls=%fused_computation.17 | convolution fusion | flops 6470696960 | bytes 17039360 | tf_op jit(solution)/shard_map/dot_general | solution.py:22
  24.9 0.4 multiply_reduce_fusion.3
  25.5 0.6 convert_reduce_fusion.1
  26.3 0.7 pad_maximum_fusion.4
  27.0 0.8 copy.25
  27.9 0.5 exp.20
  28.4 1.0 copy.26
  29.4 79.8 %psum.14 = f32[100]{0:T(128)S(1)} all-reduce(f32[100]{0:T(128)} %convert_reduce_fusion.1), channel_id=1, replica_groups=mesh['blk'=16,'dp'=16] {'blk','dp'}, use_global_device_ids=true, to_apply=%region_4.0 | all-reduce | flops 100 | bytes 800 | tf_op jit(solution)/shard_map/psum | solution.py:119
  109.2 0.5 maximum_divide_fusion
  109.7 1.2 convert_reduce_fusion
  110.9 0.9 select_reduce_fusion.5
  111.7 3.0 fusion.30
  114.8 2.6 select_reduce_fusion
  117.4 3.2 multiply_reduce_fusion
  120.7 2.4 multiply_reduce_fusion.2
  123.1 0.5 convolution_multiply_fusion
  123.7 2.8 fusion.6
  126.6 9.3 %convolution_convert_fusion = bf16[1024,3072]{1,0:T(8,128)(2,1)} fusion(bf16[1024,1024]{1,0:T(8,128)(2,1)S(1)} %fusion.6, bf16[1024,1024]{1,0:T(8,128)(2,1)S(1)} %bitcast.86, bf16[1024,1024]{1,0:T(8,128)(2,1)S(1)} %bitcast.80, bf16[1024,1024]{1,0:T(8,128)(2,1)S(1)} %bitcast.84), kind=kOutput, calls=%fused_computation.6 | convolution fusion | flops 6464471040 | bytes 14680064 | tf_op jit(solution)/shard_map/dot_general | solution.py:60
  135.9 12.1 %copy.27 = bf16[16,64,3072]{1,2,0:T(8,128)(2,1)} copy(bf16[16,64,3072]{2,1,0:T(8,128)(2,1)} %bitcast.81) | data formatting | bytes 12582912 | tf_op jit(solution)/shard_map/reshape | solution.py:67
  148.0 0.6 convolution_convert_fusion.1
  148.6 0.4 reshape.128
  149.0 1.3 copy.28
  150.4 14.7 %pad_maximum_fusion = bf16[16,64,3584]{1,2,0:T(8,128)(2,1)} fusion(bf16[16,64,512]{1,2,0:T(8,128)(2,1)S(1)} %copy.28, bf16[16,64,3072]{1,2,0:T(8,128)(2,1)} %copy.27), kind=kLoop, calls=%fused_computation | loop fusion | flops 14680064 | bytes 14680064 | tf_op jit(solution)/shard_map/concatenate | solution.py:70
  165.3 30.3 %psum.15 = f32[2,100]{1,0:T(2,128)S(1)} all-reduce(f32[2,100]{1,0:T(2,128)S(1)} %pad_maximum_fusion.5), channel_id=1, replica_groups=mesh['blk'=16,'dp'=16] {'dp'}, use_global_device_ids=true, to_apply=%region_17.18 | all-reduce | flops 200 | bytes 1600 | tf_op jit(solution)/shard_map/psum | solution.py:173
  195.6 0.5 broadcast_subtract_fusion
  196.1 1.9 multiply_reduce_fusion.1
  198.0 103.0 %reduce-scatter.2.cloned.1.call-done = bf16[1,64,3584]{1,2,0:T(8,128)(2,1)} async-done(((bf16[16,64,3584]{1,2,0:T(8,128)(2,1)}), bf16[1,64,3584]{1,2,0:T(8,128)(2,1)}) %reduce-scatter.2.cloned.1.call-update) | async-done | bytes 458768 | tf_op jit(solution)/shard_map/reduce_scatter | solution.py:172
  301.0 1.2 slice.41
  302.2 0.5 copy.29
  302.6 0.9 slice.42
  304.0 0.6 collective-permute-start
  304.6 0.7 divide_bitcast_fusion
  305.4 5.6 %collective-permute-done = bf16[64,8,224]{2,1,0:T(8,128)(2,1)S(1)} collective-permute-done((bf16[64,8,224]{2,1,0:T(8,128)(2,1)S(1)}, bf16[64,8,224]{2,1,0:T(8,128)(2,1)S(1)}, u32[]{:S(2)}, u32[]{:S(2)}) %collective-permute-start) | collective-permute-done | bytes 229408 | tf_op jit(solution)/shard_map/ppermute | solution.py:90
  311.0 0.3 reshape.129
  311.7 1.7 collective-permute-start.1
  313.6 3.2 collective-permute-done.1
  316.8 3.2 collective-permute-start.2
  320.0 0.5 slice_bitcast_fusion.1
  320.6 1.7 collective-permute-done.2
  322.3 6.7 %collective-permute-start.3 = (bf16[64,1,224]{2,0,1:T(8,128)(2,1)S(1)}, bf16[64,1,224]{2,0,1:T(8,128)(2,1)S(1)}, u32[]{:S(2)}, u32[]{:S(2)}) collective-permute-start(bf16[64,1,224]{2,0,1:T(8,128)(2,1)S(1)} %dynamic-slice_convert_fusion.2), channel_id=1, source_target_pairs={{0,128},{16,144},{32,160},{48,176},{64,192},{80,208},{96,224},{112... | collective-permute-start | bytes 86024 | tf_op jit(solution)/shard_map/ppermute | solution.py:90
  329.0 0.6 add_reduce_fusion
  329.6 1.4 collective-permute-done.3
  331.0 0.6 slice_bitcast_fusion
  331.7 0.7 reshape.132
  (79 shorter events, 2.3 us)
Async XLA Ops:
  7.2 17.8 %copy-start = (bf16[1024,512]{1,0:T(8,128)(2,1)S(1)}, bf16[1024,512]{1,0:T(8,128)(2,1)}, u32[]{:S(2)}) copy-start(bf16[1024,512]{1,0:T(8,128)(2,1)} %param.10) | copy-start | bytes 3145732
  7.2 102.5 %all-gather.2.cloned.1.call-start = ((), (), s32[]{:S(2)}) async-start(), calls=%async_computation.1 | async-start | bytes 2506752 | tf_op jit(solution)/shard_map/all_gather | solution.py:118
  10.6 1.6 copy-start.2
  10.6 4.9 %copy-start.23 = (bf16[3072,1024]{1,0:T(8,128)(2,1)S(1)}, bf16[3072,1024]{1,0:T(8,128)(2,1)}, u32[]{:S(2)}) copy-start(bf16[3072,1024]{1,0:T(8,128)(2,1)} %param.9) | copy-start | bytes 18874372
  11.5 13.4 %copy-start.5 = (bf16[64,16,1024]{2,1,0:T(8,128)(2,1)}, bf16[64,16,1024]{2,1,0:T(8,128)(2,1)S(1)}, u32[]{:S(2)}) copy-start(bf16[64,16,1024]{2,1,0:T(8,128)(2,1)S(1)} %concatenate.30) | copy-start | bytes 6291460
  11.9 13.0 %copy-start.7 = (bf16[64,16,1024]{2,1,0:T(8,128)(2,1)}, bf16[64,16,1024]{2,1,0:T(8,128)(2,1)S(1)}, u32[]{:S(2)}) copy-start(bf16[64,16,1024]{2,1,0:T(8,128)(2,1)S(1)} %concatenate.33) | copy-start | bytes 6291460
  15.5 9.8 %copy-start.9 = (bf16[1,64,512]{2,1,0:T(8,128)(2,1)S(1)}, bf16[1,64,512]{2,1,0:T(8,128)(2,1)}, u32[]{:S(2)}) copy-start(bf16[1,64,512]{2,1,0:T(8,128)(2,1)} %param.11) | copy-start | bytes 196612
  15.5 10.0 %copy-start.24 = (s32[1,64]{1,0:T(1,128)S(1)}, s32[1,64]{1,0:T(1,128)}, u32[]{:S(2)}) copy-start(s32[1,64]{1,0:T(1,128)} %param.12) | copy-start | bytes 772
  15.5 12.3 %copy-start.25 = (f32[100]{0:T(128)S(1)}, f32[100]{0:T(128)}, u32[]{:S(2)}) copy-start(f32[100]{0:T(128)} %param.13) | copy-start | bytes 1204
  15.5 93.6 %copy-start.19 = (f32[100]{0:T(128)S(1)}, f32[100]{0:T(128)}, u32[]{:S(2)}) copy-start(f32[100]{0:T(128)} %param.15) | copy-start | bytes 1204
  15.5 95.3 %copy-start.18 = (f32[100]{0:T(128)S(1)}, f32[100]{0:T(128)}, u32[]{:S(2)}) copy-start(f32[100]{0:T(128)} %param.14) | copy-start | bytes 1204
  25.3 3.0 copy-start.13
  27.0 274.0 %reduce-scatter.2.cloned.1.call-start = ((), (), s32[]{:S(2)}) async-start(), calls=%async_computation.2 | async-start | bytes 15597568 | tf_op jit(solution)/shard_map/reduce_scatter | solution.py:172
  109.2 5.6 %copy-start.21 = (f32[100]{0:T(128)}, f32[100]{0:T(128)S(1)}, u32[]{:S(2)}) copy-start(f32[100]{0:T(128)S(1)} %psum.14) | copy-start | bytes 1204
  117.4 3.3 copy-start.14
  117.4 6.3 %copy-start.3 = (f32[1024,1024]{1,0:T(8,128)S(1)}, f32[1024,1024]{1,0:T(8,128)}, u32[]{:S(2)}) copy-start(f32[1024,1024]{1,0:T(8,128)} %get-tuple-element.34) | copy-start | bytes 12582916
  120.6 2.9 copy-start.4
  123.0 0.7 copy-start.11
  123.1 0.7 copy-start.16
  123.1 3.5 %copy-start.6 = (bf16[64,16,1024]{2,1,0:T(8,128)(2,1)S(1)}, bf16[64,16,1024]{2,1,0:T(8,128)(2,1)}, u32[]{:S(2)}) copy-start(bf16[64,16,1024]{2,1,0:T(8,128)(2,1)} %copy-done.5) | copy-start | bytes 6291460
  123.1 3.5 %copy-start.8 = (bf16[64,16,1024]{2,1,0:T(8,128)(2,1)S(1)}, bf16[64,16,1024]{2,1,0:T(8,128)(2,1)}, u32[]{:S(2)}) copy-start(bf16[64,16,1024]{2,1,0:T(8,128)(2,1)} %copy-done.7) | copy-start | bytes 6291460
  135.9 12.1 %copy-start.12 = (f32[64,512]{1,0:T(8,128)S(1)}, f32[64,512]{1,0:T(8,128)}, u32[]{:S(2)}) copy-start(f32[64,512]{1,0:T(8,128)} %copy-done.11) | copy-start | bytes 393220
  135.9 12.1 %copy-start.15 = (f32[64]{0:T(128)S(1)}, f32[64]{0:T(128)}, u32[]{:S(2)}) copy-start(f32[64]{0:T(128)} %copy-done.13) | copy-start | bytes 772
  135.9 12.1 %copy-start.17 = (f32[64]{0:T(128)S(1)}, f32[64]{0:T(128)}, u32[]{:S(2)}) copy-start(f32[64]{0:T(128)} %copy-done.16) | copy-start | bytes 772
  165.2 30.4 %copy-start.20 = (f32[100]{0:T(128)S(1)}, f32[100]{0:T(128)}, u32[]{:S(2)}) copy-start(f32[100]{0:T(128)} %param.15) | copy-start | bytes 1204
  165.2 30.4 %copy-start.22 = (f32[100]{0:T(128)S(1)}, f32[100]{0:T(128)}, u32[]{:S(2)}) copy-start(f32[100]{0:T(128)} %copy-done.21) | copy-start | bytes 1204
  165.2 31.0 %copy-start.10 = (bf16[1,64,512]{2,1,0:T(8,128)(2,1)S(1)}, bf16[1,64,512]{2,1,0:T(8,128)(2,1)}, u32[]{:S(2)}) copy-start(bf16[1,64,512]{2,1,0:T(8,128)(2,1)} %param.11) | copy-start | bytes 196612
  303.6 28.9 %copy-start.1 = (bf16[1024,512]{1,0:T(8,128)(2,1)S(1)}, bf16[1024,512]{1,0:T(8,128)(2,1)}, u32[]{:S(2)}) copy-start(bf16[1024,512]{1,0:T(8,128)(2,1)} %param.10) | copy-start | bytes 3145732
  304.0 7.0 %collective-permute-start = (bf16[64,8,224]{2,1,0:T(8,128)(2,1)S(1)}, bf16[64,8,224]{2,1,0:T(8,128)(2,1)S(1)}, u32[]{:S(2)}, u32[]{:S(2)}) collective-permute-start(bf16[64,8,224]{2,1,0:T(8,128)(2,1)S(1)} %fusion.17), channel_id=1, source_target_pairs={{0,16},{16,0},{32,48},{48,32},{64,80},{80,64},{96,112},{112,96},{1... | collective-permute-start | bytes 688136 | tf_op jit(solution)/shard_map/ppermute | solution.py:90
  311.7 5.1 %collective-permute-start.1 = (bf16[64,4,224]{2,0,1:T(8,128)(2,1)S(1)}, bf16[64,4,224]{2,0,1:T(8,128)(2,1)S(1)}, u32[]{:S(2)}, u32[]{:S(2)}) collective-permute-start(bf16[64,4,224]{2,0,1:T(8,128)(2,1)S(1)} %bitcast.92), channel_id=1, source_target_pairs={{0,32},{16,48},{32,0},{48,16},{64,96},{80,112},{96,64},{112,80},{1... | collective-permute-start | bytes 344072 | tf_op jit(solution)/shard_map/ppermute | solution.py:90
  316.8 5.5 %collective-permute-start.2 = (bf16[64,2,224]{2,0,1:T(8,128)(2,1)S(1)}, bf16[64,2,224]{2,0,1:T(8,128)(2,1)S(1)}, u32[]{:S(2)}, u32[]{:S(2)}) collective-permute-start(bf16[64,2,224]{2,0,1:T(8,128)(2,1)S(1)} %fusion.22), channel_id=1, source_target_pairs={{0,64},{16,80},{32,96},{48,112},{64,0},{80,16},{96,32},{112,48},{1... | collective-permute-start | bytes 172040 | tf_op jit(solution)/shard_map/ppermute | solution.py:90
  322.3 8.7 %collective-permute-start.3 = (bf16[64,1,224]{2,0,1:T(8,128)(2,1)S(1)}, bf16[64,1,224]{2,0,1:T(8,128)(2,1)S(1)}, u32[]{:S(2)}, u32[]{:S(2)}) collective-permute-start(bf16[64,1,224]{2,0,1:T(8,128)(2,1)S(1)} %dynamic-slice_convert_fusion.2), channel_id=1, source_target_pairs={{0,128},{16,144},{32,160},{48,176},{64,192},{80,208},{96,224},{112... | collective-permute-start | bytes 86024 | tf_op jit(solution)/shard_map/ppermute | solution.py:90
Sparse Core Ops, SparseCore 0:
  27.1 77.2 all-gather.1
  165.3 135.6 reduce-scatter.1
